TPU v7x, 128 devices: a whole 4x4x4 slice. The times are simulated.
128 devices in a mesh: dp: 8 (over z, core), expert: 16 (over x, y).
Axes of the slice: x: 4, y: 4, z: 4, core: 2. Of those that a mesh axis runs over, the one named last changes fastest.
Arguments:
- inputs: bfloat16 [16384, 3584], P(('dp', 'expert')), may hold values from -6 to 6
- out_grad: bfloat16 [16384, 3584], P(('dp', 'expert')), may hold values from -6 to 6
- expert_ids: int32 [16384, 2], P(('dp', 'expert')), may hold values from 0 to 15, all different within a row; in each aligned block of 128 rows (0 to 127, 128 to 255, ...) at most 24 rows name the same one
- gates: bfloat16 [16384, 2], P(('dp', 'expert')), may hold values from 0.099609375 to 1
- w_gate: bfloat16 [16, 1024, 3584], P('expert'), may hold values from -0.09375 to 0.09375
- w_up: bfloat16 [16, 1024, 3584], P('expert'), may hold values from -0.09375 to 0.09375
- w_down: bfloat16 [16, 1024, 3584], P('expert'), may hold values from -0.1875 to 0.1875
Outputs:
- input_grad: bfloat16 [16384, 3584], P(('dp', 'expert'))
- gate_grad: bfloat16 [16384, 2], P(('dp', 'expert'))
- grad_gate: bfloat16 [16, 1024, 3584], P('expert', 'dp')
- grad_up: bfloat16 [16, 1024, 3584], P('expert', 'dp')
- grad_down: bfloat16 [16, 1024, 3584], P('expert', 'dp')
Inputs may be any that keep to these rules, and one draw needn't show every extreme that they name: `expert_ids`: within the 128 rows of one device, no expert is named by more than 24 pairs, and in every draw some device names some expert exactly 24 times; a token's 2 experts differ.
All inputs are finite; a program needn't handle non-finite values.
Results may differ from a plain program's by a relative error of at most 0.013.
Values may be sent and summed in bfloat16 or wider, within the bound.
No kernel may reach another device: no remote copies, remote signals or barrier semaphores. Data moves between devices by JAX's collectives and lax.ppermute only.
A program may use at most 192 MiB of HBM per device.

v0:
```python
import jax
import jax.numpy as jnp
from jax import lax
from jax.sharding import PartitionSpec as P


def build_tables(expert_ids, expert_count, capacity):
    token_count, top_count = expert_ids.shape
    flat_ids = expert_ids.reshape(-1)
    columns = jnp.arange(expert_count, dtype=jnp.int32)
    onehot = (flat_ids[:, None] == columns[None, :]).astype(jnp.int32)
    earlier = jnp.cumsum(onehot, axis=0) - onehot
    position = jnp.sum(earlier * onehot, axis=1)
    slot_index = flat_ids * capacity + position
    slot_range = jnp.arange(expert_count * capacity, dtype=jnp.int32)
    pair_table = (slot_index[:, None] == slot_range[None, :]).astype(jnp.bfloat16)
    token_table = jnp.sum(
        pair_table.reshape(token_count, top_count, -1).astype(jnp.float32), axis=1
    ).astype(jnp.bfloat16)
    return (pair_table, token_table)


def contract_rows(left, right):
    return lax.dot_general(
        left, right, (((0,), (0,)), ((), ())), preferred_element_type=jnp.float32
    )


def times_weight(rows, weight):
    return lax.dot_general(
        rows, weight, (((1,), (1,)), ((), ())), preferred_element_type=jnp.float32
    )


def shards(inputs, out_grad, expert_ids, gates, w_gate, w_up, w_down):
    token_count, width = inputs.shape
    top_count = expert_ids.shape[1]
    expert_count = lax.axis_size("expert")
    capacity = 3 * token_count * top_count // (2 * expert_count)
    pair_table, token_table = build_tables(expert_ids, expert_count, capacity)
    sent_inputs = (
        contract_rows(token_table, inputs)
        .astype(jnp.bfloat16)
        .reshape(expert_count, capacity, width)
    )
    sent_grads = (
        contract_rows(token_table, out_grad)
        .astype(jnp.bfloat16)
        .reshape(expert_count, capacity, width)
    )
    sent_gates = (
        jnp.dot(gates.reshape(-1), pair_table, preferred_element_type=jnp.float32)
        .astype(jnp.bfloat16)
        .reshape(expert_count, capacity)
    )
    recv_inputs, recv_grads, recv_gates = (
        lax.all_to_all(sent_inputs, "expert", split_axis=0, concat_axis=0, tiled=True),
        lax.all_to_all(sent_grads, "expert", split_axis=0, concat_axis=0, tiled=True),
        lax.all_to_all(sent_gates, "expert", split_axis=0, concat_axis=0, tiled=True),
    )
    row_inputs = recv_inputs.reshape(-1, width)
    row_out_grads = recv_grads.reshape(-1, width)
    gate_col = recv_gates.reshape(-1).astype(jnp.float32)[:, None]
    gate_matrix = w_gate[0]
    up_matrix = w_up[0]
    down_matrix = w_down[0]
    hidden_gate = times_weight(row_inputs, gate_matrix)
    hidden_up = times_weight(row_inputs, up_matrix)
    sigma = jax.nn.sigmoid(hidden_gate)
    activation = (hidden_gate * sigma * hidden_up).astype(jnp.bfloat16)
    scaled = (gate_col * row_out_grads.astype(jnp.float32)).astype(jnp.bfloat16)
    raw_grad = times_weight(row_out_grads, down_matrix)
    act_grad = gate_col * raw_grad
    gate_hidden = (act_grad * hidden_up * sigma * (1.0 + hidden_gate * (1.0 - sigma))).astype(
        jnp.bfloat16
    )
    up_hidden = (act_grad * hidden_gate * sigma).astype(jnp.bfloat16)
    row_back = (
        jnp.dot(gate_hidden, gate_matrix, preferred_element_type=jnp.float32)
        + jnp.dot(up_hidden, up_matrix, preferred_element_type=jnp.float32)
    ).astype(jnp.bfloat16)
    expert_out = jnp.dot(activation, down_matrix, preferred_element_type=jnp.float32)
    pair_value = jnp.sum(row_out_grads.astype(jnp.float32) * expert_out, axis=1)
    pair_value = pair_value.astype(jnp.bfloat16).reshape(expert_count, capacity)
    back_rows, back_values = (
        lax.all_to_all(
            row_back.reshape(expert_count, capacity, width),
            "expert",
            split_axis=0,
            concat_axis=0,
            tiled=True,
        ),
        lax.all_to_all(pair_value, "expert", split_axis=0, concat_axis=0, tiled=True),
    )
    input_grad = jnp.dot(
        token_table, back_rows.reshape(-1, width), preferred_element_type=jnp.float32
    ).astype(jnp.bfloat16)
    gate_grad = (
        jnp.dot(pair_table, back_values.reshape(-1), preferred_element_type=jnp.float32)
        .astype(jnp.bfloat16)
        .reshape(token_count, top_count)
    )
    joint_sum = lax.psum_scatter(
        jnp.concatenate(
            [
                contract_rows(gate_hidden, row_inputs),
                contract_rows(up_hidden, row_inputs),
                contract_rows(activation, scaled),
            ],
            axis=1,
        ).astype(jnp.bfloat16),
        "dp",
        scatter_dimension=0,
        tiled=True,
    ).astype(jnp.float32)
    grad_gate = joint_sum[:, :width]
    grad_up = joint_sum[:, width : 2 * width]
    grad_down = joint_sum[:, 2 * width :]
    return (
        input_grad,
        gate_grad,
        grad_gate.astype(jnp.bfloat16)[None],
        grad_up.astype(jnp.bfloat16)[None],
        grad_down.astype(jnp.bfloat16)[None],
    )


def solution(mesh):
    in_specs = (
        P(("dp", "expert"), None),
        P(("dp", "expert"), None),
        P(("dp", "expert"), None),
        P(("dp", "expert"), None),
        P("expert", None, None),
        P("expert", None, None),
        P("expert", None, None),
    )
    out_specs = (
        P(("dp", "expert"), None),
        P(("dp", "expert"), None),
        P("expert", "dp", None),
        P("expert", "dp", None),
        P("expert", "dp", None),
    )
    return jax.shard_map(shards, mesh=mesh, in_specs=in_specs, out_specs=out_specs, check_vma=False)
```

profile of v0, /device:TPU:1, one launch (start us, length us, event | category | flops | bytes accessed | tf_op | source)
XLA Modules:
  0.0 290.2 jit_solution(8965833570983489896)
XLA Ops:
  7.2 0.9 copy.39
  8.3 0.8 copy.43
  9.3 0.6 reduce-window.6
  10.2 0.3 convolution_reduce_fusion
  10.5 0.7 all_to_all.25
  11.2 7.6 %all-to-all-start = ((bf16[16,1,24]{2,1,0:T(2,128)(2,1)}), bf16[16,1,24]{2,1,0:T(2,128)(2,1)S(1)}, u32[]{:S(2)}, u32[]{:S(2)}) async-start(bf16[16,1,24]{2,1,0:T(2,128)(2,1)} %all_to_all.25), calls=%async_computation | async-start | bytes 16384 | tf_op jit(solution)/shard_map/all_to_all | solution.py:59
  19.0 0.7 multiply_add_fusion.1
  19.8 2.4 convolution_convert_fusion.3
  22.2 2.9 all-to-all-done
  25.1 4.6 %all-to-all-start.2 = ((bf16[16,24,3584]{2,1,0:T(8,128)(2,1)}), bf16[16,24,3584]{2,1,0:T(8,128)(2,1)}, u32[]{:S(2)}, u32[]{:S(2)}) async-start(bf16[16,24,3584]{2,1,0:T(8,128)(2,1)} %bitcast.78), calls=%async_computation.2 | async-start | bytes 5505024 | tf_op jit(solution)/shard_map/all_to_all | solution.py:57
  29.7 2.5 convolution_convert_fusion.4
  32.2 30.0 %all-to-all-done.2 = bf16[16,24,3584]{2,1,0:T(8,128)(2,1)} async-done(((bf16[16,24,3584]{2,1,0:T(8,128)(2,1)}), bf16[16,24,3584]{2,1,0:T(8,128)(2,1)}, u32[]{:S(2)}, u32[]{:S(2)}) %all-to-all-start.2) | async-done | bytes 2752544 | tf_op jit(solution)/shard_map/all_to_all | solution.py:57
  62.2 6.2 %all-to-all-start.1 = ((bf16[16,24,3584]{2,1,0:T(8,128)(2,1)}), bf16[16,24,3584]{2,1,0:T(8,128)(2,1)}, u32[]{:S(2)}, u32[]{:S(2)}) async-start(bf16[16,24,3584]{2,1,0:T(8,128)(2,1)} %bitcast.1), calls=%async_computation.1 | async-start | bytes 5505024 | tf_op jit(solution)/shard_map/all_to_all | solution.py:58
  68.5 8.1 %fusion.2 = f32[384,1024]{1,0:T(8,128)} fusion(bf16[384,3584]{1,0:T(8,128)(2,1)} %bitcast.5, bf16[1,1024,3584]{2,1,0:T(8,128)(2,1)} %param.11), kind=kOutput, calls=%fused_computation.6 | convolution fusion | flops 2818572288 | bytes 11665408 | tf_op jit(solution)/shard_map/dot_general | solution.py:30
  76.7 23.3 %all-to-all-done.1 = bf16[16,24,3584]{2,1,0:T(8,128)(2,1)} async-done(((bf16[16,24,3584]{2,1,0:T(8,128)(2,1)}), bf16[16,24,3584]{2,1,0:T(8,128)(2,1)}, u32[]{:S(2)}, u32[]{:S(2)}) %all-to-all-start.1) | async-done | bytes 2752544 | tf_op jit(solution)/shard_map/all_to_all | solution.py:58
  100.0 6.3 %fusion.26 = f32[384,1024]{1,0:T(8,128)S(1)} fusion(bf16[384,3584]{1,0:T(8,128)(2,1)} %bitcast.2, bf16[1,1024,3584]{2,1,0:T(8,128)(2,1)} %param.13, f32[384]{0:T(512)S(1)} %reshape.112), kind=kOutput, calls=%fused_computation.30 | convolution fusion | flops 2818965504 | bytes 11666944 | tf_op jit(solution)/shard_map/dot_general | solution.py:30
  106.3 7.5 %multiply_convert_fusion = (bf16[384,1024]{1,0:T(8,128)(2,1)S(1)}, bf16[384,1024]{1,0:T(8,128)(2,1)S(1)}, bf16[384,1024]{1,0:T(8,128)(2,1)S(1)}) fusion(f32[384,1024]{1,0:T(8,128)S(1)} %copy-done.3, f32[384,1024]{1,0:T(8,128)S(1)} %fusion.26, bf16[384,3584]{1,0:T(8,128)(2,1)} %bitcast.5, bf16[1,1024,3584]{2,1,0:T(8,128)(2,1)} %param.12), kind=kOutput, calls=%fused_computation.26 | convolution fusion | flops 2824863744 | bytes 15597568 | tf_op jit(solution)/shard_map/dot_general | solution.py:30
  113.8 8.0 %convolution_convert_fusion = bf16[1024,3584]{1,0:T(8,128)(2,1)} fusion(bf16[384,1024]{1,0:T(8,128)(2,1)S(1)} %get-tuple-element.25, bf16[384,3584]{1,0:T(8,128)(2,1)} %bitcast.2, f32[384]{0:T(512)S(1)} %reshape.112), kind=kOutput, calls=%fused_computation.1 | convolution fusion | flops 2826371072 | bytes 10880512 | tf_op jit(solution)/shard_map/dot_general | solution.py:24
  121.8 7.8 %convolution_convert_fusion.1 = bf16[1024,3584]{1,0:T(8,128)(2,1)} fusion(bf16[384,1024]{1,0:T(8,128)(2,1)S(1)} %get-tuple-element.27, bf16[384,3584]{1,0:T(8,128)(2,1)} %bitcast.5), kind=kOutput, calls=%fused_computation.2 | convolution fusion | flops 2822242304 | bytes 10878976 | tf_op jit(solution)/shard_map/dot_general | solution.py:24
  129.6 7.9 %convolution_convert_fusion.2 = bf16[1024,3584]{1,0:T(8,128)(2,1)} fusion(bf16[384,1024]{1,0:T(8,128)(2,1)S(1)} %get-tuple-element.26, bf16[384,3584]{1,0:T(8,128)(2,1)} %bitcast.5), kind=kOutput, calls=%fused_computation.3 | convolution fusion | flops 2822242304 | bytes 10878976 | tf_op jit(solution)/shard_map/dot_general | solution.py:24
  137.4 19.6 %pad_maximum_fusion = bf16[1024,10752]{1,0:T(8,128)(2,1)} fusion(bf16[1024,3584]{1,0:T(8,128)(2,1)} %convolution_convert_fusion, bf16[1024,3584]{1,0:T(8,128)(2,1)} %convolution_convert_fusion.1, bf16[1024,3584]{1,0:T(8,128)(2,1)} %convolution_convert_fusion.2), kind=kLoop, calls=%fused_computation | loop fusion | flops 66060288 | bytes 44040192 | tf_op jit(solution)/shard_map/concatenate | solution.py:104
  157.1 7.0 %fusion.23 = bf16[384]{0:T(512)(128)(2,1)S(1)} fusion(bf16[384,1024]{1,0:T(8,128)(2,1)S(1)} %get-tuple-element.25, bf16[1,1024,3584]{2,1,0:T(8,128)(2,1)} %param.13, bf16[384,3584]{1,0:T(8,128)(2,1)} %bitcast.2), kind=kOutput, calls=%fused_computation.25 | convolution fusion | flops 2822700544 | bytes 10879744 | tf_op jit(solution)/shard_map/dot_general | solution.py:82
  164.0 0.7 convert_element_type.95
  164.7 8.9 %all-to-all-start.4 = ((bf16[16,1,24]{2,1,0:T(2,128)(2,1)}), bf16[16,1,24]{2,1,0:T(2,128)(2,1)S(1)}, u32[]{:S(2)}, u32[]{:S(2)}) async-start(bf16[16,1,24]{2,1,0:T(2,128)(2,1)} %convert_element_type.95), calls=%async_computation.4 | async-start | bytes 16384 | tf_op jit(solution)/shard_map/all_to_all | solution.py:93
  173.6 5.4 %fusion = f32[384,3584]{1,0:T(8,128)S(1)} fusion(bf16[384,1024]{1,0:T(8,128)(2,1)S(1)} %get-tuple-element.26, bf16[1,1024,3584]{2,1,0:T(8,128)(2,1)} %param.11), kind=kOutput, calls=%fused_computation.4 | convolution fusion | flops 2818572288 | bytes 13631488 | tf_op jit(solution)/shard_map/dot_general | solution.py:79
  179.0 7.7 %fusion.17 = bf16[384,3584]{1,0:T(8,128)(2,1)} fusion(f32[384,3584]{1,0:T(8,128)S(1)} %fusion, bf16[384,1024]{1,0:T(8,128)(2,1)S(1)} %get-tuple-element.27, bf16[1,1024,3584]{2,1,0:T(8,128)(2,1)} %param.12), kind=kOutput, calls=%fused_computation.19 | convolution fusion | flops 2821324800 | bytes 16384000 | tf_op jit(solution)/shard_map/dot_general | solution.py:80
  186.7 6.7 %all-to-all-start.3 = ((bf16[16,24,3584]{2,1,0:T(8,128)(2,1)}), bf16[16,24,3584]{2,1,0:T(8,128)(2,1)}, u32[]{:S(2)}, u32[]{:S(2)}) async-start(bf16[16,24,3584]{2,1,0:T(8,128)(2,1)} %bitcast.79), calls=%async_computation.3 | async-start | bytes 5505024 | tf_op jit(solution)/shard_map/all_to_all | solution.py:86
  194.0 0.6 copy.46
  194.6 30.4 %all-to-all-done.3 = bf16[16,24,3584]{2,1,0:T(8,128)(2,1)} async-done(((bf16[16,24,3584]{2,1,0:T(8,128)(2,1)}), bf16[16,24,3584]{2,1,0:T(8,128)(2,1)}, u32[]{:S(2)}, u32[]{:S(2)}) %all-to-all-start.3) | async-done | bytes 2752544 | tf_op jit(solution)/shard_map/all_to_all | solution.py:86
  225.0 3.7 %convolution_convert_fusion.5 = bf16[128,3584]{1,0:T(8,128)(2,1)} fusion(bf16[128,384]{1,0:T(8,128)(2,1)S(1)} %fusion.31, bf16[384,3584]{1,0:T(8,128)(2,1)} %bitcast.9), kind=kOutput, calls=%fused_computation.23 | convolution fusion | flops 352780288 | bytes 3768320 | tf_op jit(solution)/shard_map/dot_general | solution.py:95
  228.7 51.4 %reduce-scatter.2.cloned.1.call-done = bf16[128,10752]{1,0:T(8,128)(2,1)} async-done(((bf16[1024,10752]{1,0:T(8,128)(2,1)}), bf16[128,10752]{1,0:T(8,128)(2,1)}) %reduce-scatter.2.cloned.1.call-update) | async-done | bytes 2752528 | tf_op jit(solution)/shard_map/reduce_scatter | solution.py:103
  280.1 3.3 %slice_bitcast_fusion = (bf16[1,128,3584]{2,1,0:T(8,128)(2,1)}, bf16[1,128,3584]{2,1,0:T(8,128)(2,1)}, bf16[1,128,3584]{2,1,0:T(8,128)(2,1)}) fusion(bf16[128,10752]{1,0:T(8,128)(2,1)} %reduce-scatter.2.cloned.1.call-done), kind=kLoop, calls=%fused_computation.32 | loop fusion | bytes 5505024 | tf_op jit(solution)/shard_map/broadcast_in_dim | solution.py:124
  (30 shorter events, 1.8 us)
Async XLA Ops:
  7.2 12.6 %copy-start = (bf16[128,3584]{1,0:T(8,128)(2,1)S(1)}, bf16[128,3584]{1,0:T(8,128)(2,1)}, u32[]{:S(2)}) copy-start(bf16[128,3584]{1,0:T(8,128)(2,1)} %param.7) | copy-start | bytes 2752516
  11.2 13.9 %all-to-all-start = ((bf16[16,1,24]{2,1,0:T(2,128)(2,1)}), bf16[16,1,24]{2,1,0:T(2,128)(2,1)S(1)}, u32[]{:S(2)}, u32[]{:S(2)}) async-start(bf16[16,1,24]{2,1,0:T(2,128)(2,1)} %all_to_all.25), calls=%async_computation | async-start | bytes 16384 | tf_op jit(solution)/shard_map/all_to_all | solution.py:59
  25.1 4.6 %copy-start.2 = (bf16[128,3584]{1,0:T(8,128)(2,1)S(1)}, bf16[128,3584]{1,0:T(8,128)(2,1)}, u32[]{:S(2)}) copy-start(bf16[128,3584]{1,0:T(8,128)(2,1)} %param.8) | copy-start | bytes 2752516
  25.1 37.0 %all-to-all-start.2 = ((bf16[16,24,3584]{2,1,0:T(8,128)(2,1)}), bf16[16,24,3584]{2,1,0:T(8,128)(2,1)}, u32[]{:S(2)}, u32[]{:S(2)}) async-start(bf16[16,24,3584]{2,1,0:T(8,128)(2,1)} %bitcast.78), calls=%async_computation.2 | async-start | bytes 5505024 | tf_op jit(solution)/shard_map/all_to_all | solution.py:57
  62.2 37.8 %all-to-all-start.1 = ((bf16[16,24,3584]{2,1,0:T(8,128)(2,1)}), bf16[16,24,3584]{2,1,0:T(8,128)(2,1)}, u32[]{:S(2)}, u32[]{:S(2)}) async-start(bf16[16,24,3584]{2,1,0:T(8,128)(2,1)} %bitcast.1), calls=%async_computation.1 | async-start | bytes 5505024 | tf_op jit(solution)/shard_map/all_to_all | solution.py:58
  68.4 211.7 %reduce-scatter.2.cloned.1.call-start = ((), (), s32[]{:S(2)}) async-start(), calls=%async_computation.6 | async-start | bytes 24772608 | tf_op jit(solution)/shard_map/reduce_scatter | solution.py:103
  100.0 6.3 %copy-start.3 = (f32[384,1024]{1,0:T(8,128)S(1)}, f32[384,1024]{1,0:T(8,128)}, u32[]{:S(2)}) copy-start(f32[384,1024]{1,0:T(8,128)} %fusion.2) | copy-start | bytes 4718596
  164.7 21.9 %all-to-all-start.4 = ((bf16[16,1,24]{2,1,0:T(2,128)(2,1)}), bf16[16,1,24]{2,1,0:T(2,128)(2,1)S(1)}, u32[]{:S(2)}, u32[]{:S(2)}) async-start(bf16[16,1,24]{2,1,0:T(2,128)(2,1)} %convert_element_type.95), calls=%async_computation.4 | async-start | bytes 16384 | tf_op jit(solution)/shard_map/all_to_all | solution.py:93
  186.7 38.3 %all-to-all-start.3 = ((bf16[16,24,3584]{2,1,0:T(8,128)(2,1)}), bf16[16,24,3584]{2,1,0:T(8,128)(2,1)}, u32[]{:S(2)}, u32[]{:S(2)}) async-start(bf16[16,24,3584]{2,1,0:T(8,128)(2,1)} %bitcast.79), calls=%async_computation.3 | async-start | bytes 5505024 | tf_op jit(solution)/shard_map/all_to_all | solution.py:86
  225.0 58.4 %copy-start.1 = (bf16[128,3584]{1,0:T(8,128)(2,1)S(1)}, bf16[128,3584]{1,0:T(8,128)(2,1)}, u32[]{:S(2)}) copy-start(bf16[128,3584]{1,0:T(8,128)(2,1)} %param.7) | copy-start | bytes 2752516
Sparse Core Ops, SparseCore 0:
  157.2 122.8 reduce-scatter.1
where the time goes:
time: 291 us; the launch traced here: 290 us
  waiting for transfers between devices  138 us (47%)
  matrix products  74.6 us (26%)
  starting transfers between devices  34 us (12%)
  other arithmetic  21.2 us (7%)
  between operations  14.2 us (5%)
  local copies, waits for them, and re-layouts  8.18 us (3%)
    reduce_scatter x1, waiting for transfers between devices, shards(): lax.psum_scatter(jnp.concatenate([contract_rows(gate_hidden, row_inputs),...  51.4 us
    all_to_all x1, waiting for transfers between devices, shards(): lax.all_to_all(row_back.reshape(expert_count, capacity, width), 'expert',...  30.4 us
    all_to_all x1, waiting for transfers between devices, shards(): lax.all_to_all(sent_inputs, 'expert', split_axis=0, concat_axis=0, tiled=...  30 us
    dot_general x5, matrix products, contract_rows(): lax.dot_general(left, right, (((0,), (0,)), ((), ())), preferred_element_...  28.6 us
    all_to_all x1, waiting for transfers between devices, shards(): lax.all_to_all(sent_grads, 'expert', split_axis=0, concat_axis=0, tiled=T...  23.3 us
    dot_general x3, matrix products, times_weight(): lax.dot_general(rows, weight, (((1,), (1,)), ((), ())), preferred_element...  21.9 us
    concatenate x1, other arithmetic, shards(): jnp.concatenate([contract_rows(gate_hidden, row_inputs), contract_rows(up...  19.6 us
    all_to_all x1, starting transfers between devices, shards(): lax.all_to_all(pair_value, 'expert', split_axis=0, concat_axis=0, tiled=T...  8.86 us
  transfers between devices with their start and end apart: 6, of which 5 were waited for; matrix products, arithmetic and copies ran while one was open for 14% of the time, Pallas kernels for 0%

commit v1 on v0

v1 whole, which is shorter than its diff:
```python
import jax
import jax.numpy as jnp
from jax import lax
from jax.sharding import PartitionSpec as P


def build_tables(expert_ids, expert_count, capacity):
    token_count, top_count = expert_ids.shape
    flat_ids = expert_ids.reshape(-1)
    columns = jnp.arange(expert_count, dtype=jnp.int32)
    onehot = (flat_ids[:, None] == columns[None, :]).astype(jnp.int32)
    earlier = jnp.cumsum(onehot, axis=0) - onehot
    position = jnp.sum(earlier * onehot, axis=1)
    slot_index = flat_ids * capacity + position
    slot_range = jnp.arange(expert_count * capacity, dtype=jnp.int32)
    pair_table = (slot_index[:, None] == slot_range[None, :]).astype(jnp.bfloat16)
    token_table = jnp.sum(
        pair_table.reshape(token_count, top_count, -1).astype(jnp.float32), axis=1
    ).astype(jnp.bfloat16)
    return (pair_table, token_table)


def contract_rows(left, right):
    return lax.dot_general(
        left, right, (((0,), (0,)), ((), ())), preferred_element_type=jnp.float32
    )


def times_weight(rows, weight):
    return lax.dot_general(
        rows, weight, (((1,), (1,)), ((), ())), preferred_element_type=jnp.float32
    )


LANES = 128


def shards(inputs, out_grad, expert_ids, gates, w_gate, w_up, w_down):
    token_count, width = inputs.shape
    top_count = expert_ids.shape[1]
    expert_count = lax.axis_size("expert")
    capacity = 3 * token_count * top_count // (2 * expert_count)
    slots = expert_count * capacity
    pair_table, token_table = build_tables(expert_ids, expert_count, capacity)

    both = jnp.concatenate([inputs, out_grad], axis=1)
    sent_rows = contract_rows(token_table, both).astype(jnp.bfloat16)
    sent_gates = jnp.dot(
        gates.reshape(-1), pair_table, preferred_element_type=jnp.float32
    ).astype(jnp.bfloat16)
    gate_block = jnp.zeros((slots, LANES), jnp.bfloat16).at[:, 0].set(sent_gates)
    packed = jnp.concatenate([sent_rows, gate_block], axis=1)
    recv = lax.all_to_all(
        packed.reshape(expert_count, capacity, -1),
        "expert",
        split_axis=0,
        concat_axis=0,
        tiled=True,
    ).reshape(slots, -1)
    row_inputs = recv[:, :width]
    row_out_grads = recv[:, width : 2 * width]
    gate_col = recv[:, 2 * width : 2 * width + 1].astype(jnp.float32)

    gate_matrix = w_gate[0]
    up_matrix = w_up[0]
    down_matrix = w_down[0]
    hidden_gate = times_weight(row_inputs, gate_matrix)
    hidden_up = times_weight(row_inputs, up_matrix)
    raw_grad = times_weight(row_out_grads, down_matrix)
    sigma = jax.nn.sigmoid(hidden_gate)
    activation = (hidden_gate * sigma * hidden_up).astype(jnp.bfloat16)
    scaled = (gate_col * row_out_grads.astype(jnp.float32)).astype(jnp.bfloat16)
    act_grad = gate_col * raw_grad
    gate_hidden = (act_grad * hidden_up * sigma * (1.0 + hidden_gate * (1.0 - sigma))).astype(
        jnp.bfloat16
    )
    up_hidden = (act_grad * hidden_gate * sigma).astype(jnp.bfloat16)

    def scatter(part):
        return lax.psum_scatter(
            part.astype(jnp.bfloat16), "dp", scatter_dimension=0, tiled=True
        )

    grad_gate = scatter(contract_rows(gate_hidden, row_inputs))
    grad_up = scatter(contract_rows(up_hidden, row_inputs))
    grad_down = scatter(contract_rows(activation, scaled))

    row_back = (
        jnp.dot(gate_hidden, gate_matrix, preferred_element_type=jnp.float32)
        + jnp.dot(up_hidden, up_matrix, preferred_element_type=jnp.float32)
    ).astype(jnp.bfloat16)
    pair_value = jnp.sum(activation.astype(jnp.float32) * raw_grad, axis=1).astype(
        jnp.bfloat16
    )
    value_block = jnp.zeros((slots, LANES), jnp.bfloat16).at[:, 0].set(pair_value)
    back = lax.all_to_all(
        jnp.concatenate([row_back, value_block], axis=1).reshape(
            expert_count, capacity, -1
        ),
        "expert",
        split_axis=0,
        concat_axis=0,
        tiled=True,
    ).reshape(slots, -1)
    back_rows = back[:, :width]
    back_values = back[:, width].astype(jnp.float32)
    input_grad = jnp.dot(
        token_table, back_rows, preferred_element_type=jnp.float32
    ).astype(jnp.bfloat16)
    gate_grad = (
        jnp.dot(pair_table.astype(jnp.float32), back_values, preferred_element_type=jnp.float32)
        .astype(jnp.bfloat16)
        .reshape(token_count, top_count)
    )
    return (input_grad, gate_grad, grad_gate[None], grad_up[None], grad_down[None])


def solution(mesh):
    in_specs = (
        P(("dp", "expert"), None),
        P(("dp", "expert"), None),
        P(("dp", "expert"), None),
        P(("dp", "expert"), None),
        P("expert", None, None),
        P("expert", None, None),
        P("expert", None, None),
    )
    out_specs = (
        P(("dp", "expert"), None),
        P(("dp", "expert"), None),
        P("expert", "dp", None),
        P("expert", "dp", None),
        P("expert", "dp", None),
    )
    return jax.shard_map(shards, mesh=mesh, in_specs=in_specs, out_specs=out_specs, check_vma=False)
```

time: 291 us -> 264 us (0.907)
  blocking collectives: 0 us -> 110 us
  waiting for transfers between devices: 138 us -> 81.7 us
  starting transfers between devices: 34 us -> 0.3 us
  matrix products: 74.6 us -> 49.7 us
  other arithmetic: 21.2 us -> 4.31 us
  local copies, waits for them, and re-layouts: 8.18 us -> 3.58 us
    all_to_all x0 -> x2, blocking collectives: none -> 110 us  [the longest x1 72.5 us: shards(): lax.all_to_all(packed.reshape(expert_count, capacity, -1), 'expert', spli...]
    all_to_all x5 -> x0, waiting for transfers between devices: 86.6 us -> none  [the longest x1 30.4 us: shards(): lax.all_to_all(row_back.reshape(expert_count, capacity, width), 'expert',...]
    all_to_all x5 -> x0, starting transfers between devices: 33.9 us -> none  [the longest x1 8.86 us: shards(): lax.all_to_all(pair_value, 'expert', split_axis=0, concat_axis=0, tiled=T...]
    reduce_scatter x1 -> x3, waiting for transfers between devices: 51.4 us -> 81.7 us  [scatter(): lax.psum_scatter(part.astype(jnp.bfloat16), 'dp', scatter_dimension=0, ti...]
    concatenate x1 -> x2, other arithmetic: 19.6 us -> 0.57 us  [the longest x1 0.38 us: shards(): packed = jnp.concatenate([sent_rows, gate_block], axis=1)]
    dot_general x3 -> x2, matrix products: 10.9 us -> 1.79 us  [the longest x1 1.57 us: shards(): jnp.dot(token_table, back_rows, preferred_element_type=jnp.float32)]
    dot_general x3, matrix products: 21.9 us -> 13.4 us  [times_weight(): lax.dot_general(rows, weight, (((1,), (1,)), ((), ())), preferred_element...]
    dot_general x1, matrix products: 7.66 us -> 3.29 us  [shards(): jnp.dot(up_hidden, up_matrix, preferred_element_type=jnp.float32)]
  transfers between devices with their start and end apart: 6 -> 3, of which waited for: 5 -> 2; matrix products, arithmetic and copies ran while one was open for 14% -> 11% of each run, Pallas kernels for 0% -> 0%
where the time goes in v1:
time: 264 us
  blocking collectives  110 us (42%)
  waiting for transfers between devices  81.7 us (31%)
  matrix products  49.7 us (19%)
  between operations  14 us (5%)
  other arithmetic  4.31 us (2%)
  local copies, waits for them, and re-layouts  3.58 us (1%)
    reduce_scatter x3, waiting for transfers between devices, scatter(): lax.psum_scatter(part.astype(jnp.bfloat16), 'dp', scatter_dimension=0, ti...  81.7 us
    all_to_all x1, blocking collectives, shards(): lax.all_to_all(packed.reshape(expert_count, capacity, -1), 'expert', spli...  72.5 us
    all_to_all x1, blocking collectives, shards(): lax.all_to_all(jnp.concatenate([row_back, value_block], axis=1).reshape(e...  37.9 us
    dot_general x4, matrix products, contract_rows(): lax.dot_general(left, right, (((0,), (0,)), ((), ())), preferred_element_...  25.3 us
    dot_general x3, matrix products, times_weight(): lax.dot_general(rows, weight, (((1,), (1,)), ((), ())), preferred_element...  13.4 us
    dot_general x1, matrix products, shards(): jnp.dot(gate_hidden, gate_matrix, preferred_element_type=jnp.float32)  5.7 us
  transfers between devices with their start and end apart: 3, of which 2 were waited for; matrix products, arithmetic and copies ran while one was open for 11% of the time, Pallas kernels for 0%

profile of v1, /device:TPU:1, one launch (start us, length us, event | category | flops | bytes accessed | tf_op | source)
XLA Modules:
  0.0 264.2 jit_solution(6751924032420257110)
XLA Ops:
  7.2 0.8 copy.43
  8.1 0.1 eq.45
  8.3 0.6 compare_reduce_fusion
  8.9 0.6 reduce-window.6
  9.5 0.2 slice_reduce_fusion.1
  9.8 0.1 reduce_sum.33
  10.0 0.8 copy.47
  10.8 0.1 reshape.138
  10.9 0.3 convolution_reduce_fusion
  11.2 0.7 convert_select_fusion.1
  12.0 0.7 multiply_add_fusion.1
  12.8 3.1 %convolution_convert_fusion = bf16[384,7168]{1,0:T(8,128)(2,1)S(1)} fusion(bf16[128,384]{1,0:T(8,128)(2,1)S(1)} %fusion.33, bf16[128,3584]{1,0:T(8,128)(2,1)} %param.12, bf16[128,3584]{1,0:T(8,128)(2,1)} %param.11), kind=kOutput, calls=%fused_computation.2 | convolution fusion | flops 711065600 | bytes 7438336 | tf_op jit(solution)/shard_map/dot_general | solution.py:24
  15.9 0.4 fusion.15
  16.3 72.5 %all_to_all.10 = bf16[16,24,7296]{2,1,0:T(8,128)(2,1)S(1)} all-to-all(bf16[16,24,7296]{2,1,0:T(8,128)(2,1)S(1)} %bitcast.55), channel_id=1, replica_groups=mesh['dp'=8,'expert'=16] {'expert'}, dimensions={0} | all-to-all | bytes 11206656 | tf_op jit(solution)/shard_map/all_to_all | solution.py:53
  89.0 4.2 %fusion.3 = f32[384,1024]{1,0:T(8,128)} fusion(bf16[1,1024,3584]{2,1,0:T(8,128)(2,1)S(1)} %bitcast.69, bf16[384,7296]{1,0:T(8,128)(2,1)S(1)} %bitcast.60), kind=kOutput, calls=%fused_computation.8 | convolution fusion | flops 2818572288 | bytes 11665408 | tf_op jit(solution)/shard_map/dot_general | solution.py:30
  93.2 5.4 %fusion.7 = f32[384,1024]{1,0:T(8,128)S(1)} fusion(bf16[1,1024,3584]{2,1,0:T(8,128)(2,1)} %param.16, bf16[384,7296]{1,0:T(8,128)(2,1)S(1)} %bitcast.61), kind=kOutput, calls=%fused_computation.12 | convolution fusion | flops 2818572288 | bytes 11665408 | tf_op jit(solution)/shard_map/dot_general | solution.py:30
  98.7 3.8 %multiply_reduce_fusion = (bf16[384]{0:T(512)(128)(2,1)S(1)}, bf16[384,1024]{1,0:T(8,128)(2,1)S(1)}, bf16[384,1024]{1,0:T(8,128)(2,1)S(1)}, bf16[384,1024]{1,0:T(8,128)(2,1)S(1)}) fusion(f32[384,1024]{1,0:T(8,128)S(1)} %fusion.7, f32[384,1024]{1,0:T(8,128)S(1)} %copy-done.4, f32[384]{0:T(512)S(1)} %convert_reduce_fusion, ...), kind=kOutput, calls=%fused_computation.35 | convolution fusion | flops 2826436096 | bytes 15600384 | tf_op jit(solution)/shard_map/dot_general | solution.py:30
  102.5 6.4 %convolution_convert_fusion.1 = bf16[1024,3584]{1,0:T(8,128)(2,1)} fusion(bf16[384,1024]{1,0:T(8,128)(2,1)S(1)} %get-tuple-element.50, f32[384]{0:T(512)S(1)} %convert_reduce_fusion, bf16[384,7296]{1,0:T(8,128)(2,1)S(1)} %bitcast.63), kind=kOutput, calls=%fused_computation.3 | convolution fusion | flops 2826371072 | bytes 10881024 | tf_op jit(solution)/shard_map/dot_general | solution.py:24
  108.9 0.2 reduce-scatter.6.cloned.1.call-start
  109.2 7.9 %convolution_convert_fusion.2 = bf16[1024,3584]{1,0:T(8,128)(2,1)} fusion(bf16[384,1024]{1,0:T(8,128)(2,1)S(1)} %get-tuple-element.52, bf16[384,7296]{1,0:T(8,128)(2,1)} %bitcast.64), kind=kOutput, calls=%fused_computation.4 | convolution fusion | flops 2822242304 | bytes 10878976 | tf_op jit(solution)/shard_map/dot_general | solution.py:24
  117.2 7.9 %convolution_convert_fusion.3 = bf16[1024,3584]{1,0:T(8,128)(2,1)} fusion(bf16[384,1024]{1,0:T(8,128)(2,1)S(1)} %get-tuple-element.51, bf16[384,7296]{1,0:T(8,128)(2,1)} %bitcast.65), kind=kOutput, calls=%fused_computation.5 | convolution fusion | flops 2822242304 | bytes 10878976 | tf_op jit(solution)/shard_map/dot_general | solution.py:24
  125.1 0.8 convert_select_fusion
  126.0 5.7 %fusion.1 = f32[384,3584]{1,0:T(8,128)S(1)} fusion(bf16[384,1024]{1,0:T(8,128)(2,1)} %copy-done.1, bf16[1,1024,3584]{2,1,0:T(8,128)(2,1)} %param.15), kind=kOutput, calls=%fused_computation.6 | convolution fusion | flops 2818572288 | bytes 13631488 | tf_op jit(solution)/shard_map/dot_general | solution.py:89
  131.8 3.3 %fusion.16 = bf16[384,3584]{1,0:T(8,128)(2,1)S(1)} fusion(f32[384,3584]{1,0:T(8,128)S(1)} %fusion.1, bf16[384,1024]{1,0:T(8,128)(2,1)S(1)} %copy-done.3, bf16[1,1024,3584]{2,1,0:T(8,128)(2,1)S(1)} %bitcast.71), kind=kOutput, calls=%fused_computation.20 | convolution fusion | flops 2821324800 | bytes 16384000 | tf_op jit(solution)/shard_map/dot_general | solution.py:90
  135.1 0.2 fusion.19
  135.3 37.9 %all_to_all.11 = bf16[16,24,3712]{2,1,0:T(8,128)(2,1)S(1)} all-to-all(bf16[16,24,3712]{2,1,0:T(8,128)(2,1)S(1)} %bitcast.58), channel_id=1, replica_groups=mesh['dp'=8,'expert'=16] {'expert'}, dimensions={0} | all-to-all | bytes 5701632 | tf_op jit(solution)/shard_map/all_to_all | solution.py:96
  173.4 0.2 fusion.31
  173.6 0.2 reshape.136
  173.8 0.6 copy.50
  174.4 1.6 convolution_convert_fusion.4
  176.0 31.5 %reduce-scatter.6.cloned.1.call-done = bf16[128,3584]{1,0:T(8,128)(2,1)} async-done(((bf16[1024,3584]{1,0:T(8,128)(2,1)}), bf16[128,3584]{1,0:T(8,128)(2,1)}) %reduce-scatter.6.cloned.1.call-update) | async-done | bytes 917520 | tf_op jit(solution)/shard_map/reduce_scatter | solution.py:80
  207.4 50.2 %reduce-scatter.4.cloned.1.call-done = bf16[128,3584]{1,0:T(8,128)(2,1)} async-done(((bf16[1024,3584]{1,0:T(8,128)(2,1)}), bf16[128,3584]{1,0:T(8,128)(2,1)}) %reduce-scatter.4.cloned.1.call-update) | async-done | bytes 917520 | tf_op jit(solution)/shard_map/reduce_scatter | solution.py:80
  (45 shorter events, 1.1 us)
Async XLA Ops:
  7.2 168.8 %reduce-scatter.8.cloned.1.call-start = ((), (), s32[]{:S(2)}) async-start(), calls=%async_computation.7 | async-start | bytes 8257536 | tf_op jit(solution)/shard_map/reduce_scatter | solution.py:80
  15.9 73.1 %slice-start.2 = ((s8[7340032]{0:T(1024)(128)(4,1)}), s8[3145728]{0:T(1024)(128)(4,1)S(1)}, s32[]{:S(2)}) async-start(s8[7340032]{0:T(1024)(128)(4,1)} %bitcast.68), calls=%async_computation.10 | async-start | bytes 6291456
  16.3 72.7 %slice-start.3 = ((s8[7340032]{0:T(1024)(128)(4,1)}), s8[4194304]{0:T(1024)(128)(4,1)S(1)}, s32[]{:S(2)}) async-start(s8[7340032]{0:T(1024)(128)(4,1)} %bitcast.68), calls=%async_computation.11 | async-start | bytes 8388608
  88.8 13.6 %copy-start = (bf16[16,24,7296]{2,1,0:T(8,128)(2,1)}, bf16[16,24,7296]{2,1,0:T(8,128)(2,1)S(1)}, u32[]{:S(2)}) copy-start(bf16[16,24,7296]{2,1,0:T(8,128)(2,1)S(1)} %all_to_all.10) | copy-start | bytes 16809988
  89.0 9.7 %slice-start = ((s8[7340032]{0:T(1024)(128)(4,1)}), s8[4194304]{0:T(1024)(128)(4,1)S(1)}, s32[]{:S(2)}) async-start(s8[7340032]{0:T(1024)(128)(4,1)} %bitcast.66), calls=%async_computation.8 | async-start | bytes 8388608
  93.2 5.5 %slice-start.1 = ((s8[7340032]{0:T(1024)(128)(4,1)}), s8[3145728]{0:T(1024)(128)(4,1)S(1)}, s32[]{:S(2)}) async-start(s8[7340032]{0:T(1024)(128)(4,1)} %bitcast.66), calls=%async_computation.9 | async-start | bytes 6291456
  93.2 5.5 %copy-start.4 = (f32[384,1024]{1,0:T(8,128)S(1)}, f32[384,1024]{1,0:T(8,128)}, u32[]{:S(2)}) copy-start(f32[384,1024]{1,0:T(8,128)} %fusion.3) | copy-start | bytes 4718596
  102.4 6.7 %copy-start.2 = (bf16[384,1024]{1,0:T(8,128)(2,1)}, bf16[384,1024]{1,0:T(8,128)(2,1)S(1)}, u32[]{:S(2)}) copy-start(bf16[384,1024]{1,0:T(8,128)(2,1)S(1)} %get-tuple-element.52) | copy-start | bytes 2359300
  102.4 14.7 %copy-start.1 = (bf16[384,1024]{1,0:T(8,128)(2,1)}, bf16[384,1024]{1,0:T(8,128)(2,1)S(1)}, u32[]{:S(2)}) copy-start(bf16[384,1024]{1,0:T(8,128)(2,1)S(1)} %get-tuple-element.51) | copy-start | bytes 2359300
  108.9 98.5 %reduce-scatter.6.cloned.1.call-start = ((), (), s32[]{:S(2)}) async-start(), calls=%async_computation.6 | async-start | bytes 8257536 | tf_op jit(solution)/shard_map/reduce_scatter | solution.py:80
  117.1 140.5 %reduce-scatter.4.cloned.1.call-start = ((), (), s32[]{:S(2)}) async-start(), calls=%async_computation.5 | async-start | bytes 8257536 | tf_op jit(solution)/shard_map/reduce_scatter | solution.py:80
  125.1 6.7 %slice-start.4 = ((s8[7340032]{0:T(1024)(128)(4,1)}), s8[3145728]{0:T(1024)(128)(4,1)S(1)}, s32[]{:S(2)}) async-start(s8[7340032]{0:T(1024)(128)(4,1)} %bitcast.70), calls=%async_computation.12 | async-start | bytes 6291456
  126.0 5.7 %slice-start.5 = ((s8[7340032]{0:T(1024)(128)(4,1)}), s8[4194304]{0:T(1024)(128)(4,1)S(1)}, s32[]{:S(2)}) async-start(s8[7340032]{0:T(1024)(128)(4,1)} %bitcast.70), calls=%async_computation.13 | async-start | bytes 8388608
  126.0 5.7 %copy-start.3 = (bf16[384,1024]{1,0:T(8,128)(2,1)S(1)}, bf16[384,1024]{1,0:T(8,128)(2,1)}, u32[]{:S(2)}) copy-start(bf16[384,1024]{1,0:T(8,128)(2,1)} %copy-done.2) | copy-start | bytes 2359300
Sparse Core Ops, SparseCore 0:
  109.0 47.9 reduce-scatter.7
  160.0 47.3 reduce-scatter.5
  210.4 47.1 reduce-scatter.3

commit v2 on v1

--- a/solution.py
+++ b/solution.py
@@ -76,14 +76,26 @@
     )
     up_hidden = (act_grad * hidden_gate * sigma).astype(jnp.bfloat16)
 
-    def scatter(part):
-        return lax.psum_scatter(
-            part.astype(jnp.bfloat16), "dp", scatter_dimension=0, tiled=True
+    n_z = lax.axis_size("z")
+    n_core = lax.axis_size("core")
+
+    def core_major(hidden):
+        rows = hidden.shape[0]
+        return (
+            hidden.reshape(rows, n_z, n_core, -1)
+            .transpose(0, 2, 1, 3)
+            .reshape(rows, -1)
         )
 
-    grad_gate = scatter(contract_rows(gate_hidden, row_inputs))
-    grad_up = scatter(contract_rows(up_hidden, row_inputs))
-    grad_down = scatter(contract_rows(activation, scaled))
+    def scatter(part):
+        part = part.astype(jnp.bfloat16).reshape(n_core, n_z, -1, width)
+        part = lax.psum_scatter(part, "core", scatter_dimension=0, tiled=True)
+        part = lax.psum_scatter(part, "z", scatter_dimension=1, tiled=True)
+        return part.reshape(-1, width)
+
+    grad_gate = scatter(contract_rows(core_major(gate_hidden), row_inputs))
+    grad_up = scatter(contract_rows(core_major(up_hidden), row_inputs))
+    grad_down = scatter(contract_rows(core_major(activation), scaled))
 
     row_back = (
         jnp.dot(gate_hidden, gate_matrix, preferred_element_type=jnp.float32)
@@ -116,20 +128,25 @@
 
 
 def solution(mesh):
+    n_dp = mesh.shape["dp"]
+    chip_mesh = jax.sharding.Mesh(
+        mesh.devices.reshape(n_dp // 2, 2, mesh.shape["expert"]), ("z", "core", "expert")
+    )
+    tokens = P(("z", "core", "expert"), None)
     in_specs = (
-        P(("dp", "expert"), None),
-        P(("dp", "expert"), None),
-        P(("dp", "expert"), None),
-        P(("dp", "expert"), None),
+        tokens,
+        tokens,
+        tokens,
+        tokens,
         P("expert", None, None),
         P("expert", None, None),
         P("expert", None, None),
     )
     out_specs = (
-        P(("dp", "expert"), None),
-        P(("dp", "expert"), None),
-        P("expert", "dp", None),
-        P("expert", "dp", None),
-        P("expert", "dp", None),
+        tokens,
+        tokens,
+        P("expert", ("z", "core"), None),
+        P("expert", ("z", "core"), None),
+        P("expert", ("z", "core"), None),
     )
-    return jax.shard_map(shards, mesh=mesh, in_specs=in_specs, out_specs=out_specs, check_vma=False)
+    return jax.shard_map(shards, mesh=chip_mesh, in_specs=in_specs, out_specs=out_specs, check_vma=False)

time: 264 us -> 330 us (1.25)
  waiting for transfers between devices: 81.7 us -> 121 us
  matrix products: 49.7 us -> 62.4 us
  local copies, waits for them, and re-layouts: 3.58 us -> 12.7 us
  blocking collectives: 110 us -> 114 us
    reduce_scatter x3 -> x6, waiting for transfers between devices: 81.7 us -> 121 us  [the longest x3 80 us: scatter(): part = lax.psum_scatter(part, 'z', scatter_dimension=1, tiled=True)]
    reshape x0 -> x6, local copies, waits for them, and re-layouts: none -> 9.1 us  [core_major(): hidden.reshape(rows, n_z, n_core, -1).transpose(0, 2, 1, 3)]
    dot_general x4, matrix products: 25.3 us -> 31.4 us  [contract_rows(): lax.dot_general(left, right, (((0,), (0,)), ((), ())), preferred_element_...]
    dot_general x3, matrix products: 13.4 us -> 17.4 us  [times_weight(): lax.dot_general(rows, weight, (((1,), (1,)), ((), ())), preferred_element...]
    all_to_all x1, blocking collectives: 37.9 us -> 41.9 us  [shards(): lax.all_to_all(jnp.concatenate([row_back, value_block], axis=1).reshape(e...]
  transfers between devices with their start and end apart: 3 -> 6, of which waited for: 2 -> 4; matrix products, arithmetic and copies ran while one was open for 11% -> 12% of each run, Pallas kernels for 0% -> 0%
where the time goes in v2:
time: 330 us
  waiting for transfers between devices  121 us (37%)
  blocking collectives  114 us (35%)
  matrix products  62.4 us (19%)
  between operations  14.3 us (4%)
  local copies, waits for them, and re-layouts  12.7 us (4%)
  other arithmetic  4.16 us (1%)
    reduce_scatter x3, waiting for transfers between devices, scatter(): part = lax.psum_scatter(part, 'z', scatter_dimension=1, tiled=True)  80 us
    all_to_all x1, blocking collectives, shards(): lax.all_to_all(packed.reshape(expert_count, capacity, -1), 'expert', spli...  72.5 us
    all_to_all x1, blocking collectives, shards(): lax.all_to_all(jnp.concatenate([row_back, value_block], axis=1).reshape(e...  41.9 us
    reduce_scatter x3, waiting for transfers between devices, scatter(): part = lax.psum_scatter(part, 'core', scatter_dimension=0, tiled=True)  40.7 us
    dot_general x4, matrix products, contract_rows(): lax.dot_general(left, right, (((0,), (0,)), ((), ())), preferred_element_...  31.4 us
    dot_general x3, matrix products, times_weight(): lax.dot_general(rows, weight, (((1,), (1,)), ((), ())), preferred_element...  17.4 us
    reshape x6, local copies, waits for them, and re-layouts, core_major(): hidden.reshape(rows, n_z, n_core, -1).transpose(0, 2, 1, 3)  9.1 us
  transfers between devices with their start and end apart: 6, of which 4 were waited for; matrix products, arithmetic and copies ran while one was open for 12% of the time, Pallas kernels for 0%

profile of v2, /device:TPU:1, one launch (start us, length us, event | category | flops | bytes accessed | tf_op | source)
XLA Modules:
  0.0 329.6 jit_solution(11594277903310857834)
XLA Ops:
  7.2 0.8 copy.52
  8.3 0.6 compare_reduce_fusion
  8.9 0.6 reduce-window.6
  10.0 0.8 copy.56
  11.2 0.7 convert_select_fusion.1
  12.0 0.7 multiply_add_fusion.1
  12.8 3.1 convolution_convert_fusion
  15.9 0.4 fusion.15
  16.3 72.5 %all_to_all.10 = bf16[16,24,7296]{2,1,0:T(8,128)(2,1)S(1)} all-to-all(bf16[16,24,7296]{2,1,0:T(8,128)(2,1)S(1)} %bitcast.67), channel_id=1, replica_groups=mesh['z'=4,'core'=2,'expert'=16] {'expert'}, dimensions={0} | all-to-all | bytes 11206656 | tf_op jit(solution)/shard_map/all_to_all | solution.py:53
  89.0 7.3 %fusion.3 = f32[384,1024]{1,0:T(8,128)S(1)} fusion(bf16[1,1024,3584]{2,1,0:T(8,128)(2,1)} %param.15, bf16[384,7296]{1,0:T(8,128)(2,1)S(1)} %bitcast.75), kind=kOutput, calls=%fused_computation.8 | convolution fusion | flops 2818572288 | bytes 11665408 | tf_op jit(solution)/shard_map/dot_general | solution.py:30
  96.3 4.2 %fusion.7 = f32[384,1024]{1,0:T(8,128)} fusion(bf16[1,1024,3584]{2,1,0:T(8,128)(2,1)S(1)} %bitcast.87, bf16[384,7296]{1,0:T(8,128)(2,1)S(1)} %bitcast.76), kind=kOutput, calls=%fused_computation.12 | convolution fusion | flops 2818572288 | bytes 11665408 | tf_op jit(solution)/shard_map/dot_general | solution.py:30
  100.5 6.0 %multiply_reduce_fusion = (bf16[384]{0:T(512)(128)(2,1)S(1)}, bf16[384,1024]{1,0:T(8,128)(2,1)}, bf16[384,1024]{1,0:T(8,128)(2,1)S(1)}, bf16[384,1024]{1,0:T(8,128)(2,1)S(1)}) fusion(f32[384,1024]{1,0:T(8,128)} %fusion.7, f32[384,1024]{1,0:T(8,128)S(1)} %fusion.3, f32[384]{0:T(512)S(1)} %convert_reduce_fusion, bf16[1,1024,3584]{2,1,0:T(8,128)(2,1)S(1)} %bitcast.85, ...), kind=kOutput, calls=%fused_computation.35 | convolution fusion | flops 2826436096 | bytes 15600384 | tf_op jit(solution)/shard_map/dot_general | solution.py:30
  106.4 2.6 reshape.170
  109.0 1.8 copy.61
  110.8 9.0 %convolution_convert_fusion.1 = bf16[1024,3584]{1,0:T(8,128)(2,1)} fusion(bf16[384,1024]{0,1:T(8,128)(2,1)} %bitcast.81, f32[384]{0:T(512)S(1)} %convert_reduce_fusion, bf16[384,7296]{1,0:T(8,128)(2,1)} %bitcast.78), kind=kOutput, calls=%fused_computation.3 | convolution fusion | flops 2826371072 | bytes 10880512 | tf_op jit(solution)/shard_map/dot_general | solution.py:24
  120.2 0.6 reshape.164
  120.7 1.8 copy.59
  122.5 9.6 %convolution_convert_fusion.3 = bf16[1024,3584]{1,0:T(8,128)(2,1)} fusion(bf16[384,1024]{0,1:T(8,128)(2,1)} %bitcast.83, bf16[384,7296]{1,0:T(8,128)(2,1)} %bitcast.79), kind=kOutput, calls=%fused_computation.5 | convolution fusion | flops 2822242304 | bytes 10878976 | tf_op jit(solution)/shard_map/dot_general | solution.py:24
  132.3 0.6 reshape.167
  132.8 1.8 copy.60
  134.6 9.6 %convolution_convert_fusion.2 = bf16[1024,3584]{1,0:T(8,128)(2,1)} fusion(bf16[384,1024]{0,1:T(8,128)(2,1)} %bitcast.82, bf16[384,7296]{1,0:T(8,128)(2,1)} %bitcast.80), kind=kOutput, calls=%fused_computation.4 | convolution fusion | flops 2822242304 | bytes 10878976 | tf_op jit(solution)/shard_map/dot_general | solution.py:24
  144.3 0.5 reduce-scatter.17.cloned.1.call-update
  144.9 18.0 %reduce-scatter.7.cloned.1.call-done = bf16[1,4,128,3584]{3,2,1,0:T(8,128)(2,1)} async-done(((bf16[2,4,128,3584]{3,2,1,0:T(8,128)(2,1)}), bf16[1,4,128,3584]{3,2,1,0:T(8,128)(2,1)}) %reduce-scatter.7.cloned.1.call-update) | async-done | bytes 3670032 | tf_op jit(solution)/shard_map/reduce_scatter | solution.py:92
  162.9 22.7 %reduce-scatter.11.cloned.1.call-done = bf16[1,4,128,3584]{3,2,1,0:T(8,128)(2,1)} async-done(((bf16[2,4,128,3584]{3,2,1,0:T(8,128)(2,1)}), bf16[1,4,128,3584]{3,2,1,0:T(8,128)(2,1)}) %reduce-scatter.11.cloned.1.call-update) | async-done | bytes 3670032 | tf_op jit(solution)/shard_map/reduce_scatter | solution.py:92
  185.6 0.7 convert_select_fusion
  186.4 5.2 %fusion.1 = f32[384,3584]{1,0:T(8,128)S(1)} fusion(bf16[384,1024]{1,0:T(8,128)(2,1)S(1)} %get-tuple-element.51, bf16[1,1024,3584]{2,1,0:T(8,128)(2,1)} %param.15), kind=kOutput, calls=%fused_computation.6 | convolution fusion | flops 2818572288 | bytes 13631488 | tf_op jit(solution)/shard_map/dot_general | solution.py:101
  191.7 6.3 %fusion.16 = bf16[384,3584]{1,0:T(8,128)(2,1)S(1)} fusion(f32[384,3584]{1,0:T(8,128)S(1)} %fusion.1, bf16[384,1024]{1,0:T(8,128)(2,1)S(1)} %get-tuple-element.52, bf16[1,1024,3584]{2,1,0:T(8,128)(2,1)} %param.16), kind=kOutput, calls=%fused_computation.20 | convolution fusion | flops 2821324800 | bytes 16384000 | tf_op jit(solution)/shard_map/dot_general | solution.py:102
  198.2 41.9 %all_to_all.11 = bf16[16,24,3712]{2,1,0:T(8,128)(2,1)S(1)} all-to-all(bf16[16,24,3712]{2,1,0:T(8,128)(2,1)S(1)} %bitcast.70), channel_id=1, replica_groups=mesh['z'=4,'core'=2,'expert'=16] {'expert'}, dimensions={0} | all-to-all | bytes 5701632 | tf_op jit(solution)/shard_map/all_to_all | solution.py:108
  240.6 0.6 copy.62
  241.3 1.6 convolution_convert_fusion.4
  242.8 34.7 %reduce-scatter.9.cloned.1.call-done = bf16[1,1,128,3584]{3,2,1,0:T(8,128)(2,1)} async-done(((bf16[1,4,128,3584]{3,2,1,0:T(8,128)(2,1)}), bf16[1,1,128,3584]{3,2,1,0:T(8,128)(2,1)}) %reduce-scatter.9.cloned.1.call-update) | async-done | bytes 917520 | tf_op jit(solution)/shard_map/reduce_scatter | solution.py:93
  277.5 45.3 %reduce-scatter.13.cloned.1.call-done = bf16[1,1,128,3584]{3,2,1,0:T(8,128)(2,1)} async-done(((bf16[1,4,128,3584]{3,2,1,0:T(8,128)(2,1)}), bf16[1,1,128,3584]{3,2,1,0:T(8,128)(2,1)}) %reduce-scatter.13.cloned.1.call-update) | async-done | bytes 917520 | tf_op jit(solution)/shard_map/reduce_scatter | solution.py:93
  (47 shorter events, 3.0 us)
Async XLA Ops:
  7.2 137.2 %reduce-scatter.15.cloned.1.call-start = ((), (), s32[]{:S(2)}) async-start(), calls=%async_computation.12 | async-start | bytes 11010048 | tf_op jit(solution)/shard_map/reduce_scatter | solution.py:92
  16.3 79.9 %slice-start.2 = ((s8[7340032]{0:T(1024)(128)(4,1)}), s8[4194304]{0:T(1024)(128)(4,1)S(1)}, s32[]{:S(2)}) async-start(s8[7340032]{0:T(1024)(128)(4,1)} %bitcast.86), calls=%async_computation.16 | async-start | bytes 8388608
  88.8 11.6 %copy-start = (bf16[16,24,7296]{2,1,0:T(8,128)(2,1)}, bf16[16,24,7296]{2,1,0:T(8,128)(2,1)S(1)}, u32[]{:S(2)}) copy-start(bf16[16,24,7296]{2,1,0:T(8,128)(2,1)S(1)} %all_to_all.10) | copy-start | bytes 16809988
  88.9 7.3 %slice-start.3 = ((s8[7340032]{0:T(1024)(128)(4,1)}), s8[3145728]{0:T(1024)(128)(4,1)S(1)}, s32[]{:S(2)}) async-start(s8[7340032]{0:T(1024)(128)(4,1)} %bitcast.86), calls=%async_computation.17 | async-start | bytes 6291456
  89.0 11.5 %slice-start = ((s8[7340032]{0:T(1024)(128)(4,1)}), s8[4194304]{0:T(1024)(128)(4,1)S(1)}, s32[]{:S(2)}) async-start(s8[7340032]{0:T(1024)(128)(4,1)} %bitcast.84), calls=%async_computation.14 | async-start | bytes 8388608
  96.3 4.2 %slice-start.1 = ((s8[7340032]{0:T(1024)(128)(4,1)}), s8[3145728]{0:T(1024)(128)(4,1)S(1)}, s32[]{:S(2)}) async-start(s8[7340032]{0:T(1024)(128)(4,1)} %bitcast.84), calls=%async_computation.15 | async-start | bytes 6291456
  119.9 43.0 %reduce-scatter.7.cloned.1.call-start = ((), (), s32[]{:S(2)}) async-start(), calls=%async_computation.8 | async-start | bytes 11010048 | tf_op jit(solution)/shard_map/reduce_scatter | solution.py:92
  132.2 53.4 %reduce-scatter.11.cloned.1.call-start = ((), (), s32[]{:S(2)}) async-start(), calls=%async_computation.10 | async-start | bytes 11010048 | tf_op jit(solution)/shard_map/reduce_scatter | solution.py:92
  144.3 98.6 %reduce-scatter.17.cloned.1.call-start = ((), (), s32[]{:S(2)}) async-start(), calls=%async_computation.13 | async-start | bytes 4587520 | tf_op jit(solution)/shard_map/reduce_scatter | solution.py:93
  144.8 132.7 %reduce-scatter.9.cloned.1.call-start = ((), (), s32[]{:S(2)}) async-start(), calls=%async_computation.9 | async-start | bytes 4587520 | tf_op jit(solution)/shard_map/reduce_scatter | solution.py:93
  162.9 159.9 %reduce-scatter.13.cloned.1.call-start = ((), (), s32[]{:S(2)}) async-start(), calls=%async_computation.11 | async-start | bytes 4587520 | tf_op jit(solution)/shard_map/reduce_scatter | solution.py:93
Sparse Core Ops, SparseCore 0:
  120.0 20.0 reduce-scatter.14
  142.5 20.2 reduce-scatter.6
  165.3 20.2 reduce-scatter.10
  188.4 43.8 reduce-scatter.16
  235.2 42.3 reduce-scatter.8
  280.4 42.3 reduce-scatter.12

commit v3 on v1

--- a/solution.py
+++ b/solution.py
@@ -76,14 +76,13 @@
     )
     up_hidden = (act_grad * hidden_gate * sigma).astype(jnp.bfloat16)
 
-    def scatter(part):
-        return lax.psum_scatter(
-            part.astype(jnp.bfloat16), "dp", scatter_dimension=0, tiled=True
-        )
-
-    grad_gate = scatter(contract_rows(gate_hidden, row_inputs))
-    grad_up = scatter(contract_rows(up_hidden, row_inputs))
-    grad_down = scatter(contract_rows(activation, scaled))
+    lefts = jnp.stack([gate_hidden, up_hidden, activation])
+    rights = jnp.stack([row_inputs, row_inputs, scaled])
+    partials = lax.dot_general(
+        lefts, rights, (((1,), (1,)), ((0,), (0,))), preferred_element_type=jnp.float32
+    ).astype(jnp.bfloat16)
+    joint = lax.psum_scatter(partials, "dp", scatter_dimension=1, tiled=True)
+    grad_gate, grad_up, grad_down = joint[0], joint[1], joint[2]
 
     row_back = (
         jnp.dot(gate_hidden, gate_matrix, preferred_element_type=jnp.float32)

time: 264 us -> 256 us (0.970)
  waiting for transfers between devices: 81.7 us -> 63.1 us
  matrix products: 49.7 us -> 55.9 us
  local copies, waits for them, and re-layouts: 3.58 us -> 7.31 us
    dot_general x4 -> x1, matrix products: 25.3 us -> 3.08 us  [contract_rows(): lax.dot_general(left, right, (((0,), (0,)), ((), ())), preferred_element_...]
    reduce_scatter x3 -> x1, waiting for transfers between devices: 81.7 us -> 63.1 us  [shards(): joint = lax.psum_scatter(partials, 'dp', scatter_dimension=1, tiled=True)]
    dot_general x0 -> x1, matrix products: none -> 17.5 us  [shards(): lax.dot_general(lefts, rights, (((1,), (1,)), ((0,), (0,))), preferred_el...]
    dot_general x3, matrix products: 13.4 us -> 21.2 us  [times_weight(): lax.dot_general(rows, weight, (((1,), (1,)), ((), ())), preferred_element...]
    dot_general x1, matrix products: 3.29 us -> 6.69 us  [shards(): jnp.dot(up_hidden, up_matrix, preferred_element_type=jnp.float32)]
    slice x0 -> x1, local copies, waits for them, and re-layouts: none -> 3.32 us  [shards(): grad_gate, grad_up, grad_down = (joint[0], joint[1], joint[2])]
  transfers between devices with their start and end apart: 3 -> 1, of which waited for: 2 -> 1; matrix products, arithmetic and copies ran while one was open for 11% -> 6% of each run, Pallas kernels for 0% -> 0%
where the time goes in v3:
time: 256 us
  blocking collectives  110 us (43%)
  waiting for transfers between devices  63.1 us (25%)
  matrix products  55.9 us (22%)
  between operations  14.2 us (6%)
  local copies, waits for them, and re-layouts  7.31 us (3%)
  other arithmetic  5.04 us (2%)
    all_to_all x1, blocking collectives, shards(): lax.all_to_all(packed.reshape(expert_count, capacity, -1), 'expert', spli...  72.3 us
    reduce_scatter x1, waiting for transfers between devices, shards(): joint = lax.psum_scatter(partials, 'dp', scatter_dimension=1, tiled=True)  63.1 us
    all_to_all x1, blocking collectives, shards(): lax.all_to_all(jnp.concatenate([row_back, value_block], axis=1).reshape(e...  38 us
    dot_general x3, matrix products, times_weight(): lax.dot_general(rows, weight, (((1,), (1,)), ((), ())), preferred_element...  21.2 us
    dot_general x1, matrix products, shards(): lax.dot_general(lefts, rights, (((1,), (1,)), ((0,), (0,))), preferred_el...  17.5 us
    dot_general x1, matrix products, shards(): jnp.dot(up_hidden, up_matrix, preferred_element_type=jnp.float32)  6.69 us
    dot_general x1, matrix products, shards(): jnp.dot(gate_hidden, gate_matrix, preferred_element_type=jnp.float32)  5.33 us
  transfers between devices with their start and end apart: 1, of which 1 were waited for; matrix products, arithmetic and copies ran while one was open for 6% of the time, Pallas kernels for 0%

profile of v3, /device:TPU:1, one launch (start us, length us, event | category | flops | bytes accessed | tf_op | source)
XLA Modules:
  0.0 255.8 jit_solution(6014449917962176551)
XLA Ops:
  7.2 0.8 copy.46
  8.1 0.1 eq.45
  8.3 0.6 compare_reduce_fusion
  8.9 0.6 reduce-window.6
  9.5 0.2 slice_reduce_fusion.1
  9.8 0.1 reduce_sum.33
  10.0 0.8 copy.50
  10.8 0.1 reshape.138
  10.9 0.3 convolution_reduce_fusion
  11.2 0.7 convert_select_fusion.1
  12.0 0.7 multiply_add_fusion.1
  12.8 3.1 %convolution_convert_fusion.1 = bf16[384,7168]{1,0:T(8,128)(2,1)S(1)} fusion(bf16[128,384]{1,0:T(8,128)(2,1)S(1)} %fusion.40, bf16[128,3584]{1,0:T(8,128)(2,1)} %param.12, bf16[128,3584]{1,0:T(8,128)(2,1)} %param.11), kind=kOutput, calls=%fused_computation.3 | convolution fusion | flops 711065600 | bytes 7438336 | tf_op jit(solution)/shard_map/dot_general | solution.py:24
  15.9 0.4 fusion.20
  16.3 72.3 %all_to_all.10 = bf16[16,24,7296]{2,1,0:T(8,128)(2,1)S(1)} all-to-all(bf16[16,24,7296]{2,1,0:T(8,128)(2,1)S(1)} %bitcast.62), channel_id=1, replica_groups=mesh['dp'=8,'expert'=16] {'expert'}, dimensions={0} | all-to-all | bytes 11206656 | tf_op jit(solution)/shard_map/all_to_all | solution.py:53
  88.7 0.2 slice_bitcast_fusion
  88.9 7.4 %fusion.12 = f32[384,1024]{1,0:T(8,128)} fusion(bf16[1,1024,3584]{2,1,0:T(8,128)(2,1)} %param.16, bf16[384,7296]{1,0:T(8,128)(2,1)S(1)} %bitcast.58), kind=kOutput, calls=%fused_computation.15 | convolution fusion | flops 2818572288 | bytes 11665408 | tf_op jit(solution)/shard_map/dot_general | solution.py:30
  96.3 7.4 %fusion.8 = f32[384,1024]{1,0:T(8,128)} fusion(bf16[1,1024,3584]{2,1,0:T(8,128)(2,1)} %param.15, bf16[384,7296]{1,0:T(8,128)(2,1)S(1)} %bitcast.59), kind=kOutput, calls=%fused_computation.11 | convolution fusion | flops 2818572288 | bytes 11665408 | tf_op jit(solution)/shard_map/dot_general | solution.py:30
  103.7 0.8 fusion.25
  104.6 6.3 %multiply_reduce_fusion = (bf16[384]{0:T(512)(128)(2,1)S(1)}, bf16[384,1024]{1,0:T(8,128)(2,1)}, bf16[384,1024]{1,0:T(8,128)(2,1)}, bf16[384,1024]{1,0:T(8,128)(2,1)}) fusion(f32[384,1024]{1,0:T(8,128)} %fusion.12, f32[384,1024]{1,0:T(8,128)} %fusion.8, f32[384]{0:T(512)S(1)} %convert_reduce_fusion, bf16[1,1024,3584]{2,1,0:T(8,128)(2,1)S(1)} %bitcast.67, ...), kind=kOutput, calls=%fused_computation.41 | convolution fusion | flops 2826436096 | bytes 15600384 | tf_op jit(solution)/shard_map/dot_general | solution.py:30
  110.9 17.5 %convolution_convert_fusion = bf16[3,1024,3584]{2,1,0:T(8,128)(2,1)} fusion(bf16[1,384,3584]{2,1,0:T(8,128)(2,1)S(1)} %fusion.25, bf16[1,384,3584]{2,1,0:T(8,128)(2,1)S(1)} %slice_bitcast_fusion, bf16[1,384,1024]{2,1,0:T(8,128)(2,1)} %bitcast.70, bf16[1,384,1024]{2,1,0:T(8,128)(2,1)} %bitcast.68, bf16[1,384,1024]{2,1,0:T(8,128)(2,1)} %bitcast.69), kind=kOutput, calls=%fused_computation | convolution fusion | flops 8477343744 | bytes 29884416 | tf_op jit(solution)/shard_map/dot_general | solution.py:81
  128.5 0.7 convert_select_fusion
  129.3 0.3 copy-done.1
  129.6 5.3 %fusion.6 = f32[384,3584]{1,0:T(8,128)S(1)} fusion(bf16[384,1024]{1,0:T(8,128)(2,1)S(1)} %copy-done.1, bf16[1,1024,3584]{2,1,0:T(8,128)(2,1)} %param.15), kind=kOutput, calls=%fused_computation.9 | convolution fusion | flops 2818572288 | bytes 13631488 | tf_op jit(solution)/shard_map/dot_general | solution.py:88
  134.9 6.7 %fusion.21 = bf16[384,3584]{1,0:T(8,128)(2,1)S(1)} fusion(f32[384,3584]{1,0:T(8,128)S(1)} %fusion.6, bf16[384,1024]{1,0:T(8,128)(2,1)S(1)} %copy-done, bf16[1,1024,3584]{2,1,0:T(8,128)(2,1)} %param.16), kind=kOutput, calls=%fused_computation.23 | convolution fusion | flops 2821324800 | bytes 16384000 | tf_op jit(solution)/shard_map/dot_general | solution.py:89
  141.6 0.2 fusion.24
  141.8 38.0 %all_to_all.11 = bf16[16,24,3712]{2,1,0:T(8,128)(2,1)S(1)} all-to-all(bf16[16,24,3712]{2,1,0:T(8,128)(2,1)S(1)} %bitcast.65), channel_id=1, replica_groups=mesh['dp'=8,'expert'=16] {'expert'}, dimensions={0} | all-to-all | bytes 5701632 | tf_op jit(solution)/shard_map/all_to_all | solution.py:95
  180.0 0.2 fusion.38
  180.2 0.2 reshape.136
  180.4 0.6 copy.54
  181.0 1.6 convolution_convert_fusion.2
  182.6 63.1 %reduce-scatter.2.cloned.1.call-done = bf16[3,128,3584]{2,1,0:T(8,128)(2,1)} async-done(((bf16[3,1024,3584]{2,1,0:T(8,128)(2,1)}), bf16[3,128,3584]{2,1,0:T(8,128)(2,1)}) %reduce-scatter.2.cloned.1.call-update) | async-done | bytes 2752528 | tf_op jit(solution)/shard_map/reduce_scatter | solution.py:84
  245.6 3.3 %fusion.49 = (bf16[1,128,3584]{2,1,0:T(8,128)(2,1)}, bf16[1,128,3584]{2,1,0:T(8,128)(2,1)}, bf16[1,128,3584]{2,1,0:T(8,128)(2,1)}) fusion(bf16[3,128,3584]{2,1,0:T(8,128)(2,1)} %reduce-scatter.2.cloned.1.call-done), kind=kLoop, calls=%fused_computation.72 | loop fusion | bytes 5505024 | tf_op jit(solution)/shard_map/slice | solution.py:85
  (24 shorter events, 1.0 us)
Async XLA Ops:
  7.2 238.5 %reduce-scatter.2.cloned.1.call-start = ((), (), s32[]{:S(2)}) async-start(), calls=%async_computation.3 | async-start | bytes 24772608 | tf_op jit(solution)/shard_map/reduce_scatter | solution.py:84
  88.9 15.7 %slice-start = ((s8[7340032]{0:T(1024)(128)(4,1)}), s8[4194304]{0:T(1024)(128)(4,1)S(1)}, s32[]{:S(2)}) async-start(s8[7340032]{0:T(1024)(128)(4,1)} %bitcast.66), calls=%async_computation.4 | async-start | bytes 8388608
  96.3 8.2 %slice-start.1 = ((s8[7340032]{0:T(1024)(128)(4,1)}), s8[3145728]{0:T(1024)(128)(4,1)S(1)}, s32[]{:S(2)}) async-start(s8[7340032]{0:T(1024)(128)(4,1)} %bitcast.66), calls=%async_computation.5 | async-start | bytes 6291456
  128.4 1.1 copy-start.1
  129.6 5.3 %copy-start = (bf16[384,1024]{1,0:T(8,128)(2,1)S(1)}, bf16[384,1024]{1,0:T(8,128)(2,1)}, u32[]{:S(2)}) copy-start(bf16[384,1024]{1,0:T(8,128)(2,1)} %get-tuple-element.52) | copy-start | bytes 2359300
Sparse Core Ops, SparseCore 0:
  128.6 117.0 reduce-scatter.1

commit v4 on v3

--- a/solution.py
+++ b/solution.py
@@ -43,23 +43,24 @@
     slots = expert_count * capacity
     pair_table, token_table = build_tables(expert_ids, expert_count, capacity)
 
-    both = jnp.concatenate([inputs, out_grad], axis=1)
-    sent_rows = contract_rows(token_table, both).astype(jnp.bfloat16)
+    def dispatch(rows):
+        return lax.all_to_all(
+            rows.reshape(expert_count, capacity, -1),
+            "expert",
+            split_axis=0,
+            concat_axis=0,
+            tiled=True,
+        ).reshape(slots, -1)
+
     sent_gates = jnp.dot(
         gates.reshape(-1), pair_table, preferred_element_type=jnp.float32
     ).astype(jnp.bfloat16)
     gate_block = jnp.zeros((slots, LANES), jnp.bfloat16).at[:, 0].set(sent_gates)
-    packed = jnp.concatenate([sent_rows, gate_block], axis=1)
-    recv = lax.all_to_all(
-        packed.reshape(expert_count, capacity, -1),
-        "expert",
-        split_axis=0,
-        concat_axis=0,
-        tiled=True,
-    ).reshape(slots, -1)
+    sent_inputs = contract_rows(token_table, inputs).astype(jnp.bfloat16)
+    recv = dispatch(jnp.concatenate([sent_inputs, gate_block], axis=1))
+    row_out_grads = dispatch(contract_rows(token_table, out_grad).astype(jnp.bfloat16))
     row_inputs = recv[:, :width]
-    row_out_grads = recv[:, width : 2 * width]
-    gate_col = recv[:, 2 * width : 2 * width + 1].astype(jnp.float32)
+    gate_col = recv[:, width : width + 1].astype(jnp.float32)
 
     gate_matrix = w_gate[0]
     up_matrix = w_up[0]

time: 256 us -> 261 us (1.020)
  blocking collectives: 110 us -> 38.2 us
  waiting for transfers between devices: 63.1 us -> 110 us
  starting transfers between devices: 0.04 us -> 14.7 us
  matrix products: 55.9 us -> 61.6 us
  local copies, waits for them, and re-layouts: 7.31 us -> 12.3 us
  other arithmetic: 5.04 us -> 9.29 us
    all_to_all x1 -> x0, blocking collectives: 72.3 us -> none  [shards(): lax.all_to_all(packed.reshape(expert_count, capacity, -1), 'expert', spli...]
    all_to_all x0 -> x2, waiting for transfers between devices: none -> 46 us  [dispatch(): lax.all_to_all(rows.reshape(expert_count, capacity, -1), 'expert', split_...]
    all_to_all x0 -> x2, starting transfers between devices: none -> 14.7 us  [dispatch(): lax.all_to_all(rows.reshape(expert_count, capacity, -1), 'expert', split_...]
    dot_general x3, matrix products: 21.2 us -> 25.1 us  [times_weight(): lax.dot_general(rows, weight, (((1,), (1,)), ((), ())), preferred_element...]
    another operation x1, local copies, waits for them, and re-layouts: 0.18 us -> 3.56 us  [shards(): rights = jnp.stack([row_inputs, row_inputs, scaled])]
    convert_element_type x0 -> x1, other arithmetic: none -> 2.73 us  [shards(): scaled = (gate_col * row_out_grads.astype(jnp.float32)).astype(jnp.bfloat16)]
  transfers between devices with their start and end apart: 1 -> 3, of which waited for: 1 -> 3; matrix products, arithmetic and copies ran while one was open for 6% -> 16% of each run, Pallas kernels for 0% -> 0%
where the time goes in v4:
time: 261 us
  waiting for transfers between devices  110 us (42%)
  matrix products  61.6 us (24%)
  blocking collectives  38.2 us (15%)
  starting transfers between devices  14.7 us (6%)
  between operations  14.2 us (5%)
  local copies, waits for them, and re-layouts  12.3 us (5%)
  other arithmetic  9.29 us (4%)
    reduce_scatter x1, waiting for transfers between devices, shards(): joint = lax.psum_scatter(partials, 'dp', scatter_dimension=1, tiled=True)  64.2 us
    all_to_all x2, waiting for transfers between devices, dispatch(): lax.all_to_all(rows.reshape(expert_count, capacity, -1), 'expert', split_...  46 us
    all_to_all x1, blocking collectives, shards(): lax.all_to_all(jnp.concatenate([row_back, value_block], axis=1).reshape(e...  38.2 us
    dot_general x3, matrix products, times_weight(): lax.dot_general(rows, weight, (((1,), (1,)), ((), ())), preferred_element...  25.1 us
    dot_general x1, matrix products, shards(): lax.dot_general(lefts, rights, (((1,), (1,)), ((0,), (0,))), preferred_el...  17.5 us
    all_to_all x2, starting transfers between devices, dispatch(): lax.all_to_all(rows.reshape(expert_count, capacity, -1), 'expert', split_...  14.7 us
    dot_general x1, matrix products, shards(): jnp.dot(up_hidden, up_matrix, preferred_element_type=jnp.float32)  6.37 us
    dot_general x1, matrix products, shards(): jnp.dot(gate_hidden, gate_matrix, preferred_element_type=jnp.float32)  5.24 us
  transfers between devices with their start and end apart: 3, of which 3 were waited for; matrix products, arithmetic and copies ran while one was open for 16% of the time, Pallas kernels for 0%

profile of v4, /device:TPU:1, one launch (start us, length us, event | category | flops | bytes accessed | tf_op | source)
XLA Modules:
  0.0 260.6 jit_solution(2735442045174879674)
XLA Ops:
  7.2 0.9 copy.46
  8.3 0.6 compare_reduce_fusion
  9.0 0.6 reduce-window.6
  10.0 0.8 copy.50
  11.0 0.3 convolution_reduce_fusion
  11.2 0.7 convert_select_fusion.1
  12.1 0.7 multiply_add_fusion.1
  12.9 0.9 convolution_convert_fusion.2
  13.8 1.8 fusion.24
  15.6 7.8 %all-to-all-start = ((bf16[16,24,3712]{2,1,0:T(8,128)(2,1)}), bf16[16,24,3712]{2,1,0:T(8,128)(2,1)}, u32[]{:S(2)}, u32[]{:S(2)}) async-start(bf16[16,24,3712]{2,1,0:T(8,128)(2,1)} %bitcast.66), calls=%async_computation | async-start | bytes 5701632 | tf_op jit(solution)/shard_map/all_to_all | solution.py:47
  23.4 2.4 convolution_convert_fusion.1
  25.8 34.8 %all-to-all-done = bf16[16,24,3712]{2,1,0:T(8,128)(2,1)} async-done(((bf16[16,24,3712]{2,1,0:T(8,128)(2,1)}), bf16[16,24,3712]{2,1,0:T(8,128)(2,1)}, u32[]{:S(2)}, u32[]{:S(2)}) %all-to-all-start) | async-done | bytes 2850848 | tf_op jit(solution)/shard_map/all_to_all | solution.py:47
  60.6 7.0 %all-to-all-start.1 = ((bf16[16,24,3584]{2,1,0:T(8,128)(2,1)}), bf16[16,24,3584]{2,1,0:T(8,128)(2,1)}, u32[]{:S(2)}, u32[]{:S(2)}) async-start(bf16[16,24,3584]{2,1,0:T(8,128)(2,1)} %bitcast.68), calls=%async_computation.1 | async-start | bytes 5505024 | tf_op jit(solution)/shard_map/all_to_all | solution.py:47
  67.6 1.0 convert_reduce_fusion
  68.6 8.1 %fusion.11 = f32[384,1024]{1,0:T(8,128)} fusion(bf16[1,1024,3584]{2,1,0:T(8,128)(2,1)} %param.16, bf16[384,3712]{1,0:T(8,128)(2,1)} %bitcast.2), kind=kOutput, calls=%fused_computation.12 | convolution fusion | flops 2818572288 | bytes 11665408 | tf_op jit(solution)/shard_map/dot_general | solution.py:30
  76.7 8.1 %fusion.7 = f32[384,1024]{1,0:T(8,128)} fusion(bf16[1,1024,3584]{2,1,0:T(8,128)(2,1)} %param.15, bf16[384,3712]{1,0:T(8,128)(2,1)} %bitcast.2), kind=kOutput, calls=%fused_computation.8 | convolution fusion | flops 2818572288 | bytes 11665408 | tf_op jit(solution)/shard_map/dot_general | solution.py:30
  84.8 3.6 %slice_bitcast_fusion = bf16[1,384,3584]{2,1,0:T(8,128)(2,1)} fusion(bf16[384,3712]{1,0:T(8,128)(2,1)} %bitcast.2), kind=kLoop, calls=%fused_computation.34 | loop fusion | bytes 5505024 | tf_op jit(solution)/shard_map/stack | solution.py:81
  88.4 11.3 %all-to-all-done.1 = bf16[16,24,3584]{2,1,0:T(8,128)(2,1)} async-done(((bf16[16,24,3584]{2,1,0:T(8,128)(2,1)}), bf16[16,24,3584]{2,1,0:T(8,128)(2,1)}, u32[]{:S(2)}, u32[]{:S(2)}) %all-to-all-start.1) | async-done | bytes 2752544 | tf_op jit(solution)/shard_map/all_to_all | solution.py:47
  99.7 2.7 %fusion.23 = bf16[1,384,3584]{2,1,0:T(8,128)(2,1)S(1)} fusion(f32[384]{0:T(512)S(1)} %convert_reduce_fusion, bf16[1,384,3584]{2,1,0:T(8,128)(2,1)} %bitcast.63), kind=kLoop, calls=%fused_computation.24 | loop fusion | flops 4128768 | bytes 5506560 | tf_op jit(solution)/shard_map/convert_element_type | solution.py:73
  102.5 8.9 %multiply_reduce_fusion = (bf16[384]{0:T(512)(128)(2,1)S(1)}, bf16[384,1024]{1,0:T(8,128)(2,1)}, bf16[384,1024]{1,0:T(8,128)(2,1)}, bf16[384,1024]{1,0:T(8,128)(2,1)S(1)}) fusion(f32[384,1024]{1,0:T(8,128)S(1)} %copy-done.6, f32[384,1024]{1,0:T(8,128)S(1)} %copy-done.7, f32[384]{0:T(512)S(1)} %convert_reduce_fusion, bf16[384,3584]{1,0:T(8,128)(2,1)} %bitcast.4, ...), kind=kOutput, calls=%fused_computation.37 | convolution fusion | flops 2826436096 | bytes 15599872 | tf_op jit(solution)/shard_map/dot_general | solution.py:30
  111.4 17.5 %convolution_convert_fusion = bf16[3,1024,3584]{2,1,0:T(8,128)(2,1)} fusion(bf16[1,384,3584]{2,1,0:T(8,128)(2,1)S(1)} %fusion.23, bf16[1,384,3584]{2,1,0:T(8,128)(2,1)S(1)} %copy-done.3, bf16[1,384,1024]{2,1,0:T(8,128)(2,1)} %bitcast.71, bf16[1,384,1024]{2,1,0:T(8,128)(2,1)S(1)} %bitcast.69, bf16[1,384,1024]{2,1,0:T(8,128)(2,1)} %bitcast.70), kind=kOutput, calls=%fused_computation | convolution fusion | flops 8477343744 | bytes 29884416 | tf_op jit(solution)/shard_map/dot_general | solution.py:82
  128.9 0.7 convert_select_fusion
  129.8 0.3 copy-done.5
  130.0 5.2 %fusion.5 = f32[384,3584]{1,0:T(8,128)S(1)} fusion(bf16[384,1024]{1,0:T(8,128)(2,1)S(1)} %copy-done.5, bf16[1,1024,3584]{2,1,0:T(8,128)(2,1)} %param.15), kind=kOutput, calls=%fused_computation.6 | convolution fusion | flops 2818572288 | bytes 13631488 | tf_op jit(solution)/shard_map/dot_general | solution.py:89
  135.3 6.4 %fusion.20 = bf16[384,3584]{1,0:T(8,128)(2,1)S(1)} fusion(f32[384,3584]{1,0:T(8,128)S(1)} %fusion.5, bf16[384,1024]{1,0:T(8,128)(2,1)S(1)} %get-tuple-element.52, bf16[1,1024,3584]{2,1,0:T(8,128)(2,1)} %param.16), kind=kOutput, calls=%fused_computation.20 | convolution fusion | flops 2821324800 | bytes 16384000 | tf_op jit(solution)/shard_map/dot_general | solution.py:90
  141.9 38.2 %all_to_all.15 = bf16[16,24,3712]{2,1,0:T(8,128)(2,1)S(1)} all-to-all(bf16[16,24,3712]{2,1,0:T(8,128)(2,1)S(1)} %bitcast.67), channel_id=1, replica_groups=mesh['dp'=8,'expert'=16] {'expert'}, dimensions={0} | all-to-all | bytes 5701632 | tf_op jit(solution)/shard_map/all_to_all | solution.py:96
  180.1 1.5 copy-done.2
  181.7 0.2 fusion.34
  182.1 0.6 copy.54
  182.8 3.5 %convolution_convert_fusion.3 = bf16[128,3584]{1,0:T(8,128)(2,1)} fusion(bf16[128,384]{1,0:T(8,128)(2,1)S(1)} %fusion.36, bf16[384,3712]{1,0:T(8,128)(2,1)} %bitcast.65), kind=kOutput, calls=%fused_computation.25 | convolution fusion | flops 352780288 | bytes 3768320 | tf_op jit(solution)/shard_map/dot_general | solution.py:107
  186.3 64.2 %reduce-scatter.2.cloned.1.call-done = bf16[3,128,3584]{2,1,0:T(8,128)(2,1)} async-done(((bf16[3,1024,3584]{2,1,0:T(8,128)(2,1)}), bf16[3,128,3584]{2,1,0:T(8,128)(2,1)}) %reduce-scatter.2.cloned.1.call-update) | async-done | bytes 2752528 | tf_op jit(solution)/shard_map/reduce_scatter | solution.py:85
  250.4 3.3 %fusion.44 = (bf16[1,128,3584]{2,1,0:T(8,128)(2,1)}, bf16[1,128,3584]{2,1,0:T(8,128)(2,1)}, bf16[1,128,3584]{2,1,0:T(8,128)(2,1)}) fusion(bf16[3,128,3584]{2,1,0:T(8,128)(2,1)} %reduce-scatter.2.cloned.1.call-done), kind=kLoop, calls=%fused_computation.67 | loop fusion | bytes 5505024 | tf_op jit(solution)/shard_map/slice | solution.py:86
  (35 shorter events, 1.9 us)
Async XLA Ops:
  7.2 5.7 %copy-start = (bf16[128,3584]{1,0:T(8,128)(2,1)S(1)}, bf16[128,3584]{1,0:T(8,128)(2,1)}, u32[]{:S(2)}) copy-start(bf16[128,3584]{1,0:T(8,128)(2,1)} %param.11) | copy-start | bytes 2752516
  15.6 7.8 %copy-start.4 = (bf16[128,3584]{1,0:T(8,128)(2,1)S(1)}, bf16[128,3584]{1,0:T(8,128)(2,1)}, u32[]{:S(2)}) copy-start(bf16[128,3584]{1,0:T(8,128)(2,1)} %param.12) | copy-start | bytes 2752516
  15.6 45.0 %all-to-all-start = ((bf16[16,24,3712]{2,1,0:T(8,128)(2,1)}), bf16[16,24,3712]{2,1,0:T(8,128)(2,1)}, u32[]{:S(2)}, u32[]{:S(2)}) async-start(bf16[16,24,3712]{2,1,0:T(8,128)(2,1)} %bitcast.66), calls=%async_computation | async-start | bytes 5701632 | tf_op jit(solution)/shard_map/all_to_all | solution.py:47
  60.6 39.1 %all-to-all-start.1 = ((bf16[16,24,3584]{2,1,0:T(8,128)(2,1)}), bf16[16,24,3584]{2,1,0:T(8,128)(2,1)}, u32[]{:S(2)}, u32[]{:S(2)}) async-start(bf16[16,24,3584]{2,1,0:T(8,128)(2,1)} %bitcast.68), calls=%async_computation.1 | async-start | bytes 5505024 | tf_op jit(solution)/shard_map/all_to_all | solution.py:47
  67.6 182.9 %reduce-scatter.2.cloned.1.call-start = ((), (), s32[]{:S(2)}) async-start(), calls=%async_computation.4 | async-start | bytes 24772608 | tf_op jit(solution)/shard_map/reduce_scatter | solution.py:85
  99.7 2.7 %copy-start.6 = (f32[384,1024]{1,0:T(8,128)S(1)}, f32[384,1024]{1,0:T(8,128)}, u32[]{:S(2)}) copy-start(f32[384,1024]{1,0:T(8,128)} %fusion.11) | copy-start | bytes 4718596
  99.7 2.7 %copy-start.7 = (f32[384,1024]{1,0:T(8,128)S(1)}, f32[384,1024]{1,0:T(8,128)}, u32[]{:S(2)}) copy-start(f32[384,1024]{1,0:T(8,128)} %fusion.7) | copy-start | bytes 4718596
  102.4 8.9 %copy-start.3 = (bf16[1,384,3584]{2,1,0:T(8,128)(2,1)S(1)}, bf16[1,384,3584]{2,1,0:T(8,128)(2,1)}, u32[]{:S(2)}) copy-start(bf16[1,384,3584]{2,1,0:T(8,128)(2,1)} %slice_bitcast_fusion) | copy-start | bytes 8257540
  128.9 1.1 copy-start.5
  180.1 1.5 copy-start.2
  182.7 71.0 %copy-start.1 = (bf16[128,3584]{1,0:T(8,128)(2,1)S(1)}, bf16[128,3584]{1,0:T(8,128)(2,1)}, u32[]{:S(2)}) copy-start(bf16[128,3584]{1,0:T(8,128)(2,1)} %param.11) | copy-start | bytes 2752516
Sparse Core Ops, SparseCore 0:
  129.0 121.3 reduce-scatter.1

commit v5 on v3

--- a/solution.py
+++ b/solution.py
@@ -61,36 +61,49 @@
     row_out_grads = recv[:, width : 2 * width]
     gate_col = recv[:, 2 * width : 2 * width + 1].astype(jnp.float32)
 
-    gate_matrix = w_gate[0]
-    up_matrix = w_up[0]
-    down_matrix = w_down[0]
-    hidden_gate = times_weight(row_inputs, gate_matrix)
-    hidden_up = times_weight(row_inputs, up_matrix)
-    raw_grad = times_weight(row_out_grads, down_matrix)
-    sigma = jax.nn.sigmoid(hidden_gate)
-    activation = (hidden_gate * sigma * hidden_up).astype(jnp.bfloat16)
+    n_dp = lax.axis_size("dp")
+    hidden_count = w_gate.shape[1]
+    halves = 2
+    piece = hidden_count // (n_dp * halves)
+
+    def half_of(weight, h):
+        return weight[0].reshape(n_dp, halves, piece, width)[:, h].reshape(-1, width)
+
     scaled = (gate_col * row_out_grads.astype(jnp.float32)).astype(jnp.bfloat16)
-    act_grad = gate_col * raw_grad
-    gate_hidden = (act_grad * hidden_up * sigma * (1.0 + hidden_gate * (1.0 - sigma))).astype(
-        jnp.bfloat16
-    )
-    up_hidden = (act_grad * hidden_gate * sigma).astype(jnp.bfloat16)
-
-    lefts = jnp.stack([gate_hidden, up_hidden, activation])
     rights = jnp.stack([row_inputs, row_inputs, scaled])
-    partials = lax.dot_general(
-        lefts, rights, (((1,), (1,)), ((0,), (0,))), preferred_element_type=jnp.float32
-    ).astype(jnp.bfloat16)
-    joint = lax.psum_scatter(partials, "dp", scatter_dimension=1, tiled=True)
+    row_back = None
+    pair_value = None
+    joints = []
+    for h in range(halves):
+        gate_matrix = half_of(w_gate, h)
+        up_matrix = half_of(w_up, h)
+        down_matrix = half_of(w_down, h)
+        hidden_gate = times_weight(row_inputs, gate_matrix)
+        hidden_up = times_weight(row_inputs, up_matrix)
+        raw_grad = times_weight(row_out_grads, down_matrix)
+        sigma = jax.nn.sigmoid(hidden_gate)
+        activation = (hidden_gate * sigma * hidden_up).astype(jnp.bfloat16)
+        act_grad = gate_col * raw_grad
+        gate_hidden = (
+            act_grad * hidden_up * sigma * (1.0 + hidden_gate * (1.0 - sigma))
+        ).astype(jnp.bfloat16)
+        up_hidden = (act_grad * hidden_gate * sigma).astype(jnp.bfloat16)
+        lefts = jnp.stack([gate_hidden, up_hidden, activation])
+        partials = lax.dot_general(
+            lefts, rights, (((1,), (1,)), ((0,), (0,))), preferred_element_type=jnp.float32
+        ).astype(jnp.bfloat16)
+        joints.append(lax.psum_scatter(partials, "dp", scatter_dimension=1, tiled=True))
+        back_part = jnp.dot(
+            gate_hidden, gate_matrix, preferred_element_type=jnp.float32
+        ) + jnp.dot(up_hidden, up_matrix, preferred_element_type=jnp.float32)
+        value_part = jnp.sum(activation.astype(jnp.float32) * raw_grad, axis=1)
+        row_back = back_part if row_back is None else row_back + back_part
+        pair_value = value_part if pair_value is None else pair_value + value_part
+    row_back = row_back.astype(jnp.bfloat16)
+    pair_value = pair_value.astype(jnp.bfloat16)
+    joint = jnp.concatenate(joints, axis=1)
     grad_gate, grad_up, grad_down = joint[0], joint[1], joint[2]
 
-    row_back = (
-        jnp.dot(gate_hidden, gate_matrix, preferred_element_type=jnp.float32)
-        + jnp.dot(up_hidden, up_matrix, preferred_element_type=jnp.float32)
-    ).astype(jnp.bfloat16)
-    pair_value = jnp.sum(activation.astype(jnp.float32) * raw_grad, axis=1).astype(
-        jnp.bfloat16
-    )
     value_block = jnp.zeros((slots, LANES), jnp.bfloat16).at[:, 0].set(pair_value)
     back = lax.all_to_all(
         jnp.concatenate([row_back, value_block], axis=1).reshape(

time: 256 us -> 291 us (1.14)
  waiting for transfers between devices: 63.1 us -> 130 us
  blocking collectives: 110 us -> 45.6 us
  local copies, waits for them, and re-layouts: 7.31 us -> 27.4 us
  starting transfers between devices: 0.04 us -> 8.36 us
  other arithmetic: 5.04 us -> 10.4 us
    all_to_all x1 -> x0, blocking collectives: 72.3 us -> none  [shards(): lax.all_to_all(packed.reshape(expert_count, capacity, -1), 'expert', spli...]
    all_to_all x0 -> x1, waiting for transfers between devices: none -> 71.6 us  [shards(): lax.all_to_all(packed.reshape(expert_count, capacity, -1), 'expert', spli...]
    slice x0 -> x3, local copies, waits for them, and re-layouts: none -> 14.4 us  [half_of(): weight[0].reshape(n_dp, halves, piece, width)[:, h].reshape(-1, width)]
    all_to_all x0 -> x1, starting transfers between devices: none -> 7.88 us  [shards(): lax.all_to_all(packed.reshape(expert_count, capacity, -1), 'expert', spli...]
    all_to_all x1, blocking collectives: 38 us -> 45.6 us  [shards(): lax.all_to_all(jnp.concatenate([row_back, value_block], axis=1).reshape(e...]
    reduce_scatter x1 -> x2, waiting for transfers between devices: 63.1 us -> 58 us  [shards(): lax.psum_scatter(partials, 'dp', scatter_dimension=1, tiled=True)]
    unnamed x11 -> x44, local copies, waits for them, and re-layouts: 2.47 us -> 6.61 us
    dot_general x1 -> x2, matrix products: 6.69 us -> 3.18 us  [shards(): jnp.dot(up_hidden, up_matrix, preferred_element_type=jnp.float32)]
  transfers between devices with their start and end apart: 1 -> 3, of which waited for: 1 -> 2; matrix products, arithmetic and copies ran while one was open for 6% -> 17% of each run, Pallas kernels for 0% -> 0%
where the time goes in v5:
time: 291 us
  waiting for transfers between devices  130 us (45%)
  matrix products  54.9 us (19%)
  blocking collectives  45.6 us (16%)
  local copies, waits for them, and re-layouts  27.4 us (9%)
  between operations  14.4 us (5%)
  other arithmetic  10.4 us (4%)
  starting transfers between devices  8.36 us (3%)
    all_to_all x1, waiting for transfers between devices, shards(): lax.all_to_all(packed.reshape(expert_count, capacity, -1), 'expert', spli...  71.6 us
    reduce_scatter x2, waiting for transfers between devices, shards(): lax.psum_scatter(partials, 'dp', scatter_dimension=1, tiled=True)  58 us
    all_to_all x1, blocking collectives, shards(): lax.all_to_all(jnp.concatenate([row_back, value_block], axis=1).reshape(e...  45.6 us
    dot_general x6, matrix products, times_weight(): lax.dot_general(rows, weight, (((1,), (1,)), ((), ())), preferred_element...  23.7 us
    dot_general x2, matrix products, shards(): lax.dot_general(lefts, rights, (((1,), (1,)), ((0,), (0,))), preferred_el...  17.4 us
    slice x3, local copies, waits for them, and re-layouts, half_of(): weight[0].reshape(n_dp, halves, piece, width)[:, h].reshape(-1, width)  14.4 us
    all_to_all x1, starting transfers between devices, shards(): lax.all_to_all(packed.reshape(expert_count, capacity, -1), 'expert', spli...  7.88 us
    unnamed x44, local copies, waits for them, and re-layouts  6.61 us
  transfers between devices with their start and end apart: 3, of which 2 were waited for; matrix products, arithmetic and copies ran while one was open for 17% of the time, Pallas kernels for 0%

profile of v5, /device:TPU:1, one launch (start us, length us, event | category | flops | bytes accessed | tf_op | source)
XLA Modules:
  0.0 290.7 jit_solution(8333772143720974460)
XLA Ops:
  7.2 0.8 copy.50
  10.8 0.8 copy.54
  12.8 3.1 %convolution_convert_fusion = bf16[384,7168]{1,0:T(8,128)(2,1)S(1)} fusion(bf16[128,384]{1,0:T(8,128)(2,1)S(1)} %fusion.35, bf16[128,3584]{1,0:T(8,128)(2,1)} %param.12, bf16[128,3584]{1,0:T(8,128)(2,1)} %param.11), kind=kOutput, calls=%fused_computation.2 | convolution fusion | flops 711065600 | bytes 7438336 | tf_op jit(solution)/shard_map/dot_general | solution.py:24
  15.9 2.8 fusion.3
  18.7 7.9 %all-to-all-start = ((bf16[16,24,7296]{2,1,0:T(8,128)(2,1)}), bf16[16,24,7296]{2,1,0:T(8,128)(2,1)}, u32[]{:S(2)}, u32[]{:S(2)}) async-start(bf16[16,24,7296]{2,1,0:T(8,128)(2,1)} %bitcast.61), calls=%async_computation | async-start | bytes 11206656 | tf_op jit(solution)/shard_map/all_to_all | solution.py:53
  26.8 7.1 %fusion.47 = (bf16[8,1,64,3584]{3,2,1,0:T(8,128)(2,1)}, bf16[8,1,64,3584]{3,2,1,0:T(8,128)(2,1)}) fusion(bf16[8,2,64,3584]{3,2,1,0:T(8,128)(2,1)} %bitcast.73), kind=kLoop, calls=%fused_computation.85 | loop fusion | bytes 14680064 | tf_op jit(solution)/shard_map/slice | solution.py:70
  34.0 3.7 %fusion.46 = (bf16[8,1,64,3584]{3,2,1,0:T(8,128)(2,1)}, bf16[8,1,64,3584]{3,2,1,0:T(8,128)(2,1)}) fusion(bf16[8,2,64,3584]{3,2,1,0:T(8,128)(2,1)S(1)} %bitcast.76), kind=kLoop, calls=%fused_computation.84 | loop fusion | bytes 14680064 | tf_op jit(solution)/shard_map/slice | solution.py:70
  37.7 3.7 %fusion.48 = (bf16[8,1,64,3584]{3,2,1,0:T(8,128)(2,1)}, bf16[8,1,64,3584]{3,2,1,0:T(8,128)(2,1)}) fusion(bf16[8,2,64,3584]{3,2,1,0:T(8,128)(2,1)S(1)} %bitcast.79), kind=kLoop, calls=%fused_computation.86 | loop fusion | bytes 14680064 | tf_op jit(solution)/shard_map/slice | solution.py:70
  41.3 71.6 %all-to-all-done = bf16[16,24,7296]{2,1,0:T(8,128)(2,1)} async-done(((bf16[16,24,7296]{2,1,0:T(8,128)(2,1)}), bf16[16,24,7296]{2,1,0:T(8,128)(2,1)}, u32[]{:S(2)}, u32[]{:S(2)}) %all-to-all-start) | async-done | bytes 5603360 | tf_op jit(solution)/shard_map/all_to_all | solution.py:53
  112.9 1.2 convert_reduce_fusion
  114.1 2.0 slice_bitcast_fusion
  116.0 3.5 %fusion.21 = f32[384,512]{1,0:T(8,128)S(1)} fusion(bf16[512,3584]{1,0:T(8,128)(2,1)S(1)} %bitcast.68, bf16[384,7296]{1,0:T(8,128)(2,1)} %bitcast.2), kind=kOutput, calls=%fused_computation.32 | convolution fusion | flops 1409286144 | bytes 7208960 | tf_op jit(solution)/shard_map/dot_general | solution.py:30
  119.6 3.4 %fusion.19 = f32[384,512]{1,0:T(8,128)S(1)} fusion(bf16[512,3584]{1,0:T(8,128)(2,1)S(1)} %bitcast.64, bf16[384,7296]{1,0:T(8,128)(2,1)} %bitcast.2), kind=kOutput, calls=%fused_computation.30 | convolution fusion | flops 1409286144 | bytes 7208960 | tf_op jit(solution)/shard_map/dot_general | solution.py:30
  123.0 2.7 fusion.6
  125.9 4.7 %multiply_reduce_fusion.1 = (f32[384]{0:T(512)S(1)}, bf16[384,512]{1,0:T(8,128)(2,1)S(1)}, bf16[384,512]{1,0:T(8,128)(2,1)S(1)}, bf16[384,512]{1,0:T(8,128)(2,1)S(1)}) fusion(f32[384,512]{1,0:T(8,128)S(1)} %fusion.21, f32[384,512]{1,0:T(8,128)S(1)} %fusion.19, f32[384]{0:T(512)S(1)} %convert_reduce_fusion, bf16[512,3584]{1,0:T(8,128)(2,1)S(1)} %bitcast.81, ...), kind=kOutput, calls=%fused_computation.47 | convolution fusion | flops 1413217920 | bytes 9178112 | tf_op jit(solution)/shard_map/dot_general | solution.py:30
  130.6 0.7 copy-done.10
  131.3 8.6 %convolution_convert_fusion.2 = bf16[3,512,3584]{2,1,0:T(8,128)(2,1)} fusion(bf16[1,384,3584]{2,1,0:T(8,128)(2,1)S(1)} %fusion.6, bf16[1,384,3584]{2,1,0:T(8,128)(2,1)S(1)} %slice_bitcast_fusion, bf16[1,384,512]{2,1,0:T(8,128)(2,1)S(1)} %bitcast.87, bf16[1,384,512]{2,1,0:T(8,128)(2,1)S(1)} %bitcast.82, bf16[1,384,512]{2,1,0:T(8,128)(2,1)S(1)} %bitcast.83), kind=kOutput, calls=%fused_computation.4 | convolution fusion | flops 4242800640 | bytes 17694720 | tf_op jit(solution)/shard_map/dot_general | solution.py:92
  140.2 4.6 %fusion.17 = f32[384,512]{1,0:T(8,128)S(1)} fusion(bf16[512,3584]{1,0:T(8,128)(2,1)} %bitcast.62, bf16[384,7296]{1,0:T(8,128)(2,1)} %bitcast.2), kind=kOutput, calls=%fused_computation.28 | convolution fusion | flops 1409286144 | bytes 7208960 | tf_op jit(solution)/shard_map/dot_general | solution.py:30
  144.9 3.5 %fusion.15 = f32[384,512]{1,0:T(8,128)S(1)} fusion(bf16[512,3584]{1,0:T(8,128)(2,1)S(1)} %bitcast.67, bf16[384,7296]{1,0:T(8,128)(2,1)} %bitcast.2), kind=kOutput, calls=%fused_computation.26 | convolution fusion | flops 1409286144 | bytes 7208960 | tf_op jit(solution)/shard_map/dot_general | solution.py:30
  148.5 4.0 %multiply_reduce_fusion = (f32[384]{0:T(512)S(1)}, bf16[384,512]{1,0:T(8,128)(2,1)S(1)}, bf16[384,512]{1,0:T(8,128)(2,1)S(1)}, bf16[384,512]{1,0:T(8,128)(2,1)S(1)}) fusion(f32[384,512]{1,0:T(8,128)S(1)} %fusion.17, f32[384,512]{1,0:T(8,128)S(1)} %fusion.15, f32[384]{0:T(512)S(1)} %convert_reduce_fusion, bf16[512,3584]{1,0:T(8,128)(2,1)S(1)} %bitcast.80, ...), kind=kOutput, calls=%fused_computation.45 | convolution fusion | flops 1413217920 | bytes 9178112 | tf_op jit(solution)/shard_map/dot_general | solution.py:30
  152.4 0.7 copy-done.12
  153.3 8.8 %convolution_convert_fusion.1 = bf16[3,512,3584]{2,1,0:T(8,128)(2,1)} fusion(bf16[1,384,3584]{2,1,0:T(8,128)(2,1)S(1)} %copy-done.9, bf16[1,384,3584]{2,1,0:T(8,128)(2,1)S(1)} %slice_bitcast_fusion, bf16[1,384,512]{2,1,0:T(8,128)(2,1)S(1)} %bitcast.86, bf16[1,384,512]{2,1,0:T(8,128)(2,1)S(1)} %bitcast.85, bf16[1,384,512]{2,1,0:T(8,128)(2,1)S(1)} %bitcast.84), kind=kOutput, calls=%fused_computation.3 | convolution fusion | flops 4242800640 | bytes 17694720 | tf_op jit(solution)/shard_map/dot_general | solution.py:92
  163.1 3.9 %fusion.51 = f32[384,3584]{1,0:T(8,128)S(1)} fusion(bf16[384,512]{1,0:T(8,128)(2,1)S(1)} %copy-done.13, bf16[512,3584]{1,0:T(8,128)(2,1)} %bitcast.66), kind=kOutput, calls=%fused_computation.89 | convolution fusion | flops 1409286144 | bytes 9568256 | tf_op jit(solution)/shard_map/dot_general | solution.py:96
  167.0 1.6 fusion.50
  169.2 1.6 convolution_add_fusion
  171.2 1.6 fusion.4
  173.0 45.6 %all_to_all.10 = bf16[16,24,3712]{2,1,0:T(8,128)(2,1)S(1)} all-to-all(bf16[16,24,3712]{2,1,0:T(8,128)(2,1)S(1)} %bitcast.72), channel_id=1, replica_groups=mesh['dp'=8,'expert'=16] {'expert'}, dimensions={0} | all-to-all | bytes 5701632 | tf_op jit(solution)/shard_map/all_to_all | solution.py:108
  219.9 1.6 convolution_convert_fusion.3
  221.4 1.4 constant_dynamic-update-slice_fusion.1
  222.9 58.0 %reduce-scatter.5.cloned.1.call-done = bf16[3,64,3584]{2,1,0:T(8,128)(2,1)} async-done(((bf16[3,512,3584]{2,1,0:T(8,128)(2,1)}), bf16[3,64,3584]{2,1,0:T(8,128)(2,1)}) %reduce-scatter.5.cloned.1.call-update) | async-done | bytes 1376272 | tf_op jit(solution)/shard_map/reduce_scatter | solution.py:95
  280.9 1.4 constant_dynamic-update-slice_fusion
  282.3 1.6 fusion.49
  (72 shorter events, 8.2 us)
Async XLA Ops:
  18.7 15.3 %slice-start = ((s8[7340032]{0:T(1024)(128)(4,1)}), s8[3145728]{0:T(1024)(128)(4,1)S(1)}, s32[]{:S(2)}) async-start(s8[7340032]{0:T(1024)(128)(4,1)} %bitcast.74), calls=%async_computation.6 | async-start | bytes 6291456
  18.7 94.2 %all-to-all-start = ((bf16[16,24,7296]{2,1,0:T(8,128)(2,1)}), bf16[16,24,7296]{2,1,0:T(8,128)(2,1)}, u32[]{:S(2)}, u32[]{:S(2)}) async-start(bf16[16,24,7296]{2,1,0:T(8,128)(2,1)} %bitcast.61), calls=%async_computation | async-start | bytes 11206656 | tf_op jit(solution)/shard_map/all_to_all | solution.py:53
  26.6 194.8 %reduce-scatter.3.cloned.1.call-start = ((), (), s32[]{:S(2)}) async-start(), calls=%async_computation.4 | async-start | bytes 12386304 | tf_op jit(solution)/shard_map/reduce_scatter | solution.py:95
  26.8 7.2 %slice-start.1 = ((s8[7340032]{0:T(1024)(128)(4,1)}), s8[4194304]{0:T(1024)(128)(4,1)S(1)}, s32[]{:S(2)}) async-start(s8[7340032]{0:T(1024)(128)(4,1)} %bitcast.74), calls=%async_computation.7 | async-start | bytes 8388608
  26.8 10.8 %slice-start.2 = ((s8[7340032]{0:T(1024)(128)(4,1)}), s8[4194304]{0:T(1024)(128)(4,1)S(1)}, s32[]{:S(2)}) async-start(s8[7340032]{0:T(1024)(128)(4,1)} %bitcast.77), calls=%async_computation.8 | async-start | bytes 8388608
  34.0 3.7 %slice-start.3 = ((s8[7340032]{0:T(1024)(128)(4,1)}), s8[3145728]{0:T(1024)(128)(4,1)S(1)}, s32[]{:S(2)}) async-start(s8[7340032]{0:T(1024)(128)(4,1)} %bitcast.77), calls=%async_computation.9 | async-start | bytes 6291456
  112.9 3.1 %copy-start.4 = (bf16[8,1,64,3584]{3,2,1,0:T(8,128)(2,1)S(1)}, bf16[8,1,64,3584]{3,2,1,0:T(8,128)(2,1)}, u32[]{:S(2)}) copy-start(bf16[8,1,64,3584]{3,2,1,0:T(8,128)(2,1)} %get-tuple-element.56) | copy-start | bytes 11010052
  116.0 3.6 %copy-start.1 = (bf16[8,1,64,3584]{3,2,1,0:T(8,128)(2,1)S(1)}, bf16[8,1,64,3584]{3,2,1,0:T(8,128)(2,1)}, u32[]{:S(2)}) copy-start(bf16[8,1,64,3584]{3,2,1,0:T(8,128)(2,1)} %get-tuple-element.54) | copy-start | bytes 11010052
  123.0 2.9 copy-start.7
  125.7 4.8 %copy-start.8 = (bf16[1,384,3584]{2,1,0:T(8,128)(2,1)}, bf16[1,384,3584]{2,1,0:T(8,128)(2,1)S(1)}, u32[]{:S(2)}) copy-start(bf16[1,384,3584]{2,1,0:T(8,128)(2,1)S(1)} %fusion.6) | copy-start | bytes 8257540
  130.6 0.8 copy-start.10
  140.0 140.9 %reduce-scatter.5.cloned.1.call-start = ((), (), s32[]{:S(2)}) async-start(), calls=%async_computation.5 | async-start | bytes 12386304 | tf_op jit(solution)/shard_map/reduce_scatter | solution.py:95
  140.2 4.6 %copy-start.3 = (bf16[8,1,64,3584]{3,2,1,0:T(8,128)(2,1)S(1)}, bf16[8,1,64,3584]{3,2,1,0:T(8,128)(2,1)}, u32[]{:S(2)}) copy-start(bf16[8,1,64,3584]{3,2,1,0:T(8,128)(2,1)} %get-tuple-element.53) | copy-start | bytes 11010052
  144.9 3.6 %copy-start.6 = (bf16[8,1,64,3584]{3,2,1,0:T(8,128)(2,1)S(1)}, bf16[8,1,64,3584]{3,2,1,0:T(8,128)(2,1)}, u32[]{:S(2)}) copy-start(bf16[8,1,64,3584]{3,2,1,0:T(8,128)(2,1)} %get-tuple-element.57) | copy-start | bytes 11010052
  148.4 4.9 %copy-start.9 = (bf16[1,384,3584]{2,1,0:T(8,128)(2,1)S(1)}, bf16[1,384,3584]{2,1,0:T(8,128)(2,1)}, u32[]{:S(2)}) copy-start(bf16[1,384,3584]{2,1,0:T(8,128)(2,1)} %copy-done.8) | copy-start | bytes 8257540
  152.4 0.8 copy-start.12
  152.4 0.9 copy-start.14
  162.1 1.0 copy-start.13
  163.1 3.9 %copy-start.2 = (bf16[8,1,64,3584]{3,2,1,0:T(8,128)(2,1)S(1)}, bf16[8,1,64,3584]{3,2,1,0:T(8,128)(2,1)}, u32[]{:S(2)}) copy-start(bf16[8,1,64,3584]{3,2,1,0:T(8,128)(2,1)} %get-tuple-element.54) | copy-start | bytes 11010052
  163.1 3.9 %copy-start.11 = (bf16[384,512]{1,0:T(8,128)(2,1)S(1)}, bf16[384,512]{1,0:T(8,128)(2,1)}, u32[]{:S(2)}) copy-start(bf16[384,512]{1,0:T(8,128)(2,1)} %copy-done.10) | copy-start | bytes 1179652
  167.0 2.1 copy-start
  167.0 2.2 copy-start.15
  169.2 2.1 copy-start.5
Sparse Core Ops, SparseCore 0:
  140.1 73.5 reduce-scatter.2
  216.1 64.7 reduce-scatter.4

commit v6 on v3

--- a/solution.py
+++ b/solution.py
@@ -6,18 +6,25 @@
 
 def build_tables(expert_ids, expert_count, capacity):
     token_count, top_count = expert_ids.shape
-    flat_ids = expert_ids.reshape(-1)
     columns = jnp.arange(expert_count, dtype=jnp.int32)
-    onehot = (flat_ids[:, None] == columns[None, :]).astype(jnp.int32)
-    earlier = jnp.cumsum(onehot, axis=0) - onehot
-    position = jnp.sum(earlier * onehot, axis=1)
-    slot_index = flat_ids * capacity + position
+    onehots = [
+        (expert_ids[:, k][:, None] == columns[None, :]).astype(jnp.bfloat16)
+        for k in range(top_count)
+    ]
+    rows = jnp.arange(token_count, dtype=jnp.int32)
+    before = (rows[None, :] < rows[:, None]).astype(jnp.bfloat16)
+    earlier = jnp.dot(before, sum(onehots), preferred_element_type=jnp.float32)
     slot_range = jnp.arange(expert_count * capacity, dtype=jnp.int32)
-    pair_table = (slot_index[:, None] == slot_range[None, :]).astype(jnp.bfloat16)
-    token_table = jnp.sum(
-        pair_table.reshape(token_count, top_count, -1).astype(jnp.float32), axis=1
-    ).astype(jnp.bfloat16)
-    return (pair_table, token_table)
+    pair_tables = []
+    for k in range(top_count):
+        position = jnp.sum(earlier * onehots[k].astype(jnp.float32), axis=1)
+        earlier = earlier + onehots[k].astype(jnp.float32)
+        slot_index = expert_ids[:, k] * capacity + position.astype(jnp.int32)
+        pair_tables.append(
+            (slot_index[:, None] == slot_range[None, :]).astype(jnp.bfloat16)
+        )
+    token_table = sum(pair_tables)
+    return (pair_tables, token_table)
 
 
 def contract_rows(left, right):
@@ -45,8 +52,9 @@
 
     both = jnp.concatenate([inputs, out_grad], axis=1)
     sent_rows = contract_rows(token_table, both).astype(jnp.bfloat16)
-    sent_gates = jnp.dot(
-        gates.reshape(-1), pair_table, preferred_element_type=jnp.float32
+    sent_gates = sum(
+        jnp.dot(gates[:, k], pair_table[k], preferred_element_type=jnp.float32)
+        for k in range(top_count)
     ).astype(jnp.bfloat16)
     gate_block = jnp.zeros((slots, LANES), jnp.bfloat16).at[:, 0].set(sent_gates)
     packed = jnp.concatenate([sent_rows, gate_block], axis=1)
@@ -106,11 +114,13 @@
     input_grad = jnp.dot(
         token_table, back_rows, preferred_element_type=jnp.float32
     ).astype(jnp.bfloat16)
-    gate_grad = (
-        jnp.dot(pair_table.astype(jnp.float32), back_values, preferred_element_type=jnp.float32)
-        .astype(jnp.bfloat16)
-        .reshape(token_count, top_count)
-    )
+    gate_grad = jnp.stack(
+        [
+            jnp.dot(table.astype(jnp.float32), back_values, preferred_element_type=jnp.float32)
+            for table in pair_table
+        ],
+        axis=1,
+    ).astype(jnp.bfloat16)
     return (input_grad, gate_grad, grad_gate[None], grad_up[None], grad_down[None])
 
 

time: 256 us -> 255 us (level)
  no operation moved by 1% of the time
where the time goes in v6:
time: 255 us
  blocking collectives  110 us (43%)
  waiting for transfers between devices  63.3 us (25%)
  matrix products  57.3 us (22%)
  between operations  14.2 us (6%)
  local copies, waits for them, and re-layouts  4.88 us (2%)
  other arithmetic  4.82 us (2%)
    all_to_all x1, blocking collectives, shards(): lax.all_to_all(packed.reshape(expert_count, capacity, -1), 'expert', spli...  72.3 us
    reduce_scatter x1, waiting for transfers between devices, shards(): joint = lax.psum_scatter(partials, 'dp', scatter_dimension=1, tiled=True)  63.3 us
    all_to_all x1, blocking collectives, shards(): lax.all_to_all(jnp.concatenate([row_back, value_block], axis=1).reshape(e...  38 us
    dot_general x3, matrix products, times_weight(): lax.dot_general(rows, weight, (((1,), (1,)), ((), ())), preferred_element...  21 us
    dot_general x1, matrix products, shards(): lax.dot_general(lefts, rights, (((1,), (1,)), ((0,), (0,))), preferred_el...  17.4 us
    dot_general x1, matrix products, shards(): jnp.dot(up_hidden, up_matrix, preferred_element_type=jnp.float32)  6.56 us
    dot_general x1, matrix products, shards(): jnp.dot(gate_hidden, gate_matrix, preferred_element_type=jnp.float32)  5.25 us
  transfers between devices with their start and end apart: 1, of which 1 were waited for; matrix products, arithmetic and copies ran while one was open for 6% of the time, Pallas kernels for 0%

profile of v6, /device:TPU:1, one launch (start us, length us, event | category | flops | bytes accessed | tf_op | source)
XLA Modules:
  0.0 254.8 jit_solution(873350380986572778)
XLA Ops:
  7.2 0.6 compare_reduce_fusion
  7.9 0.8 slice_bitcast_fusion.2
  8.6 0.2 fusion.58
  8.8 0.8 fusion.66
  9.5 0.9 convolution_reduce_fusion
  10.4 0.9 convolution_reduce_fusion.1
  11.3 0.7 fusion.65
  12.0 0.1 reshape.117
  12.1 3.2 %convolution_convert_fusion.1 = bf16[384,7168]{1,0:T(8,128)(2,1)S(1)} fusion(bf16[128,3584]{1,0:T(8,128)(2,1)} %param.12, bf16[128,3584]{1,0:T(8,128)(2,1)} %param.11, s32[128]{0:T(128)S(1)} %get-tuple-element.38, s32[128]{0:T(128)S(1)} %get-tuple-element.39), kind=kOutput, calls=%fused_computation.3 | convolution fusion | flops 711458816 | bytes 7341056 | tf_op jit(solution)/shard_map/dot_general | solution.py:31
  15.3 0.4 fusion.20
  15.6 72.3 %all_to_all.10 = bf16[16,24,7296]{2,1,0:T(8,128)(2,1)S(1)} all-to-all(bf16[16,24,7296]{2,1,0:T(8,128)(2,1)S(1)} %bitcast.74), channel_id=1, replica_groups=mesh['dp'=8,'expert'=16] {'expert'}, dimensions={0} | all-to-all | bytes 11206656 | tf_op jit(solution)/shard_map/all_to_all | solution.py:61
  87.9 0.1 convert_reduce_fusion
  88.0 0.2 slice_bitcast_fusion
  88.2 0.8 fusion.25
  89.0 7.4 %fusion.12 = f32[384,1024]{1,0:T(8,128)} fusion(bf16[1,1024,3584]{2,1,0:T(8,128)(2,1)} %param.16, bf16[384,7296]{1,0:T(8,128)(2,1)S(1)} %bitcast.71), kind=kOutput, calls=%fused_computation.15 | convolution fusion | flops 2818572288 | bytes 11665408 | tf_op jit(solution)/shard_map/dot_general | solution.py:37
  96.5 7.4 %fusion.8 = f32[384,1024]{1,0:T(8,128)} fusion(bf16[1,1024,3584]{2,1,0:T(8,128)(2,1)} %param.15, bf16[384,7296]{1,0:T(8,128)(2,1)S(1)} %bitcast.72), kind=kOutput, calls=%fused_computation.11 | convolution fusion | flops 2818572288 | bytes 11665408 | tf_op jit(solution)/shard_map/dot_general | solution.py:37
  103.9 6.2 %multiply_reduce_fusion = (bf16[384]{0:T(512)(128)(2,1)S(1)}, bf16[384,1024]{1,0:T(8,128)(2,1)}, bf16[384,1024]{1,0:T(8,128)(2,1)}, bf16[384,1024]{1,0:T(8,128)(2,1)S(1)}) fusion(f32[384,1024]{1,0:T(8,128)} %fusion.12, f32[384,1024]{1,0:T(8,128)} %fusion.8, f32[384]{0:T(512)S(1)} %convert_reduce_fusion, bf16[1,1024,3584]{2,1,0:T(8,128)(2,1)S(1)} %bitcast.79, ...), kind=kOutput, calls=%fused_computation.41 | convolution fusion | flops 2826436096 | bytes 15600384 | tf_op jit(solution)/shard_map/dot_general | solution.py:37
  110.1 17.4 %convolution_convert_fusion = bf16[3,1024,3584]{2,1,0:T(8,128)(2,1)} fusion(bf16[1,384,3584]{2,1,0:T(8,128)(2,1)S(1)} %fusion.25, bf16[1,384,3584]{2,1,0:T(8,128)(2,1)S(1)} %slice_bitcast_fusion, bf16[1,384,1024]{2,1,0:T(8,128)(2,1)} %bitcast.82, bf16[1,384,1024]{2,1,0:T(8,128)(2,1)S(1)} %bitcast.80, bf16[1,384,1024]{2,1,0:T(8,128)(2,1)} %bitcast.81), kind=kOutput, calls=%fused_computation | convolution fusion | flops 8477343744 | bytes 29884416 | tf_op jit(solution)/shard_map/dot_general | solution.py:89
  127.5 0.7 convert_select_fusion
  128.2 0.1 reshape.118
  128.3 0.3 copy-done
  128.6 5.2 %fusion.6 = f32[384,3584]{1,0:T(8,128)S(1)} fusion(bf16[384,1024]{1,0:T(8,128)(2,1)S(1)} %copy-done, bf16[1,1024,3584]{2,1,0:T(8,128)(2,1)} %param.15), kind=kOutput, calls=%fused_computation.9 | convolution fusion | flops 2818572288 | bytes 13631488 | tf_op jit(solution)/shard_map/dot_general | solution.py:96
  133.8 6.6 %fusion.21 = bf16[384,3584]{1,0:T(8,128)(2,1)S(1)} fusion(f32[384,3584]{1,0:T(8,128)S(1)} %fusion.6, bf16[384,1024]{1,0:T(8,128)(2,1)S(1)} %get-tuple-element.34, bf16[1,1024,3584]{2,1,0:T(8,128)(2,1)} %param.16), kind=kOutput, calls=%fused_computation.23 | convolution fusion | flops 2821324800 | bytes 16384000 | tf_op jit(solution)/shard_map/dot_general | solution.py:97
  140.4 0.2 fusion.24
  140.6 38.0 %all_to_all.11 = bf16[16,24,3712]{2,1,0:T(8,128)(2,1)S(1)} all-to-all(bf16[16,24,3712]{2,1,0:T(8,128)(2,1)S(1)} %bitcast.75), channel_id=1, replica_groups=mesh['dp'=8,'expert'=16] {'expert'}, dimensions={0} | all-to-all | bytes 5701632 | tf_op jit(solution)/shard_map/all_to_all | solution.py:103
  178.7 0.1 slice_reduce_fusion
  178.8 0.2 fusion.39
  179.0 0.2 fusion.41
  179.2 0.5 pad_maximum_fusion
  179.8 1.6 convolution_convert_fusion.2
  181.4 63.3 %reduce-scatter.2.cloned.1.call-done = bf16[3,128,3584]{2,1,0:T(8,128)(2,1)} async-done(((bf16[3,1024,3584]{2,1,0:T(8,128)(2,1)}), bf16[3,128,3584]{2,1,0:T(8,128)(2,1)}) %reduce-scatter.2.cloned.1.call-update) | async-done | bytes 2752528 | tf_op jit(solution)/shard_map/reduce_scatter | solution.py:92
  244.6 3.3 %fusion.72 = (bf16[1,128,3584]{2,1,0:T(8,128)(2,1)}, bf16[1,128,3584]{2,1,0:T(8,128)(2,1)}, bf16[1,128,3584]{2,1,0:T(8,128)(2,1)}) fusion(bf16[3,128,3584]{2,1,0:T(8,128)(2,1)} %reduce-scatter.2.cloned.1.call-done), kind=kLoop, calls=%fused_computation.98 | loop fusion | bytes 5505024 | tf_op jit(solution)/shard_map/slice | solution.py:93
  (9 shorter events, 0.1 us)
Async XLA Ops:
  7.2 237.5 %reduce-scatter.2.cloned.1.call-start = ((), (), s32[]{:S(2)}) async-start(), calls=%async_computation.3 | async-start | bytes 24772608 | tf_op jit(solution)/shard_map/reduce_scatter | solution.py:92
  89.0 14.8 %slice-start = ((s8[7340032]{0:T(1024)(128)(4,1)}), s8[4194304]{0:T(1024)(128)(4,1)S(1)}, s32[]{:S(2)}) async-start(s8[7340032]{0:T(1024)(128)(4,1)} %bitcast.78), calls=%async_computation.4 | async-start | bytes 8388608
  96.4 7.4 %slice-start.1 = ((s8[7340032]{0:T(1024)(128)(4,1)}), s8[3145728]{0:T(1024)(128)(4,1)S(1)}, s32[]{:S(2)}) async-start(s8[7340032]{0:T(1024)(128)(4,1)} %bitcast.78), calls=%async_computation.5 | async-start | bytes 6291456
  127.4 1.1 copy-start
Sparse Core Ops, SparseCore 0:
  127.6 117.0 reduce-scatter.1

commit v7 on v6

--- a/solution.py
+++ b/solution.py
@@ -7,10 +7,8 @@
 def build_tables(expert_ids, expert_count, capacity):
     token_count, top_count = expert_ids.shape
     columns = jnp.arange(expert_count, dtype=jnp.int32)
-    onehots = [
-        (expert_ids[:, k][:, None] == columns[None, :]).astype(jnp.bfloat16)
-        for k in range(top_count)
-    ]
+    onehot = (expert_ids[:, :, None] == columns[None, None, :]).astype(jnp.bfloat16)
+    onehots = [onehot[:, k] for k in range(top_count)]
     rows = jnp.arange(token_count, dtype=jnp.int32)
     before = (rows[None, :] < rows[:, None]).astype(jnp.bfloat16)
     earlier = jnp.dot(before, sum(onehots), preferred_element_type=jnp.float32)
@@ -42,6 +40,11 @@
 LANES = 128
 
 
+def lane_block(values):
+    lane = lax.broadcasted_iota(jnp.int32, (values.shape[0], LANES), 1)
+    return jnp.where(lane == 0, values[:, None], jnp.zeros((), values.dtype))
+
+
 def shards(inputs, out_grad, expert_ids, gates, w_gate, w_up, w_down):
     token_count, width = inputs.shape
     top_count = expert_ids.shape[1]
@@ -51,13 +54,15 @@
     pair_table, token_table = build_tables(expert_ids, expert_count, capacity)
 
     both = jnp.concatenate([inputs, out_grad], axis=1)
-    sent_rows = contract_rows(token_table, both).astype(jnp.bfloat16)
-    sent_gates = sum(
-        jnp.dot(gates[:, k], pair_table[k], preferred_element_type=jnp.float32)
-        for k in range(top_count)
+    per_choice = jnp.stack(
+        [jnp.concatenate([both, lane_block(gates[:, k])], axis=1) for k in range(top_count)]
+    )
+    packed = lax.dot_general(
+        jnp.stack(pair_table),
+        per_choice,
+        (((0, 1), (0, 1)), ((), ())),
+        preferred_element_type=jnp.float32,
     ).astype(jnp.bfloat16)
-    gate_block = jnp.zeros((slots, LANES), jnp.bfloat16).at[:, 0].set(sent_gates)
-    packed = jnp.concatenate([sent_rows, gate_block], axis=1)
     recv = lax.all_to_all(
         packed.reshape(expert_count, capacity, -1),
         "expert",
@@ -99,7 +104,7 @@
     pair_value = jnp.sum(activation.astype(jnp.float32) * raw_grad, axis=1).astype(
         jnp.bfloat16
     )
-    value_block = jnp.zeros((slots, LANES), jnp.bfloat16).at[:, 0].set(pair_value)
+    value_block = lane_block(pair_value)
     back = lax.all_to_all(
         jnp.concatenate([row_back, value_block], axis=1).reshape(
             expert_count, capacity, -1

time: 255 us -> 253 us (level)
  matrix products: 57.3 us -> 54.4 us
    dot_general x3 -> x1, matrix products: 4.92 us -> 1.97 us  [shards(): lax.dot_general(jnp.stack(pair_table), per_choice, (((0, 1), (0, 1)), (()...]
where the time goes in v7:
time: 253 us
  blocking collectives  110 us (43%)
  waiting for transfers between devices  63.2 us (25%)
  matrix products  54.4 us (22%)
  between operations  14.1 us (6%)
  local copies, waits for them, and re-layouts  5.36 us (2%)
  other arithmetic  5.08 us (2%)
    all_to_all x1, blocking collectives, shards(): lax.all_to_all(packed.reshape(expert_count, capacity, -1), 'expert', spli...  72.3 us
    reduce_scatter x1, waiting for transfers between devices, shards(): joint = lax.psum_scatter(partials, 'dp', scatter_dimension=1, tiled=True)  63.2 us
    all_to_all x1, blocking collectives, shards(): lax.all_to_all(jnp.concatenate([row_back, value_block], axis=1).reshape(e...  38 us
    dot_general x3, matrix products, times_weight(): lax.dot_general(rows, weight, (((1,), (1,)), ((), ())), preferred_element...  21.1 us
    dot_general x1, matrix products, shards(): lax.dot_general(lefts, rights, (((1,), (1,)), ((0,), (0,))), preferred_el...  17.3 us
    dot_general x1, matrix products, shards(): jnp.dot(up_hidden, up_matrix, preferred_element_type=jnp.float32)  6.66 us
    dot_general x1, matrix products, shards(): jnp.dot(gate_hidden, gate_matrix, preferred_element_type=jnp.float32)  5.24 us
  transfers between devices with their start and end apart: 1, of which 1 were waited for; matrix products, arithmetic and copies ran while one was open for 6% of the time, Pallas kernels for 0%

profile of v7, /device:TPU:1, one launch (start us, length us, event | category | flops | bytes accessed | tf_op | source)
XLA Modules:
  0.0 252.5 jit_solution(4775563305378821565)
XLA Ops:
  7.2 0.0 reduce-scatter.2.cloned.1.call-start
  7.2 0.7 fusion.52
  7.9 0.2 fusion.53
  8.1 0.8 slice_bitcast_fusion.2
  8.8 0.8 fusion.61
  9.6 0.1 iota_compare_fusion
  9.6 0.1 broadcast_select_fusion.2
  9.7 1.7 maximum_bitcast_fusion
  11.5 2.0 fusion
  13.4 72.3 %all_to_all.10 = bf16[16,24,7296]{2,1,0:T(8,128)(2,1)S(1)} all-to-all(bf16[16,24,7296]{2,1,0:T(8,128)(2,1)S(1)} %bitcast.93), channel_id=1, replica_groups=mesh['dp'=8,'expert'=16] {'expert'}, dimensions={0} | all-to-all | bytes 11206656 | tf_op jit(solution)/shard_map/all_to_all | solution.py:66
  85.7 0.1 convert_reduce_fusion
  85.8 0.2 slice_bitcast_fusion
  86.0 0.8 fusion.25
  86.8 0.0 slice-start
  86.8 7.4 %fusion.12 = f32[384,1024]{1,0:T(8,128)} fusion(bf16[1,1024,3584]{2,1,0:T(8,128)(2,1)} %param.12, bf16[384,7296]{1,0:T(8,128)(2,1)S(1)} %bitcast.89), kind=kOutput, calls=%fused_computation.14 | convolution fusion | flops 2818572288 | bytes 11665408 | tf_op jit(solution)/shard_map/dot_general | solution.py:35
  94.2 7.4 %fusion.8 = f32[384,1024]{1,0:T(8,128)} fusion(bf16[1,1024,3584]{2,1,0:T(8,128)(2,1)} %param.11, bf16[384,7296]{1,0:T(8,128)(2,1)S(1)} %bitcast.90), kind=kOutput, calls=%fused_computation.10 | convolution fusion | flops 2818572288 | bytes 11665408 | tf_op jit(solution)/shard_map/dot_general | solution.py:35
  101.7 6.2 %multiply_reduce_fusion = (bf16[384]{0:T(512)(128)(2,1)S(1)}, bf16[384,1024]{1,0:T(8,128)(2,1)}, bf16[384,1024]{1,0:T(8,128)(2,1)}, bf16[384,1024]{1,0:T(8,128)(2,1)S(1)}) fusion(f32[384,1024]{1,0:T(8,128)} %fusion.12, f32[384,1024]{1,0:T(8,128)} %fusion.8, f32[384]{0:T(512)S(1)} %convert_reduce_fusion, bf16[1,1024,3584]{2,1,0:T(8,128)(2,1)S(1)} %bitcast.97, ...), kind=kOutput, calls=%fused_computation.40 | convolution fusion | flops 2826436096 | bytes 15600384 | tf_op jit(solution)/shard_map/dot_general | solution.py:35
  107.9 17.3 %convolution_convert_fusion = bf16[3,1024,3584]{2,1,0:T(8,128)(2,1)} fusion(bf16[1,384,3584]{2,1,0:T(8,128)(2,1)S(1)} %fusion.25, bf16[1,384,3584]{2,1,0:T(8,128)(2,1)S(1)} %slice_bitcast_fusion, bf16[1,384,1024]{2,1,0:T(8,128)(2,1)} %bitcast.100, bf16[1,384,1024]{2,1,0:T(8,128)(2,1)S(1)} %bitcast.98, bf16[1,384,1024]{2,1,0:T(8,128)(2,1)} %bitcast.99), kind=kOutput, calls=%fused_computation | convolution fusion | flops 8477343744 | bytes 29884416 | tf_op jit(solution)/shard_map/dot_general | solution.py:94
  125.2 0.0 reduce-scatter.2.cloned.1.call-update
  125.2 0.1 broadcast_select_fusion
  125.3 1.0 copy-done
  126.3 5.2 %fusion.6 = f32[384,3584]{1,0:T(8,128)S(1)} fusion(bf16[384,1024]{1,0:T(8,128)(2,1)S(1)} %copy-done, bf16[1,1024,3584]{2,1,0:T(8,128)(2,1)} %param.11), kind=kOutput, calls=%fused_computation.8 | convolution fusion | flops 2818572288 | bytes 13631488 | tf_op jit(solution)/shard_map/dot_general | solution.py:101
  131.5 6.7 %fusion.19 = bf16[384,3584]{1,0:T(8,128)(2,1)S(1)} fusion(f32[384,3584]{1,0:T(8,128)S(1)} %fusion.6, bf16[384,1024]{1,0:T(8,128)(2,1)S(1)} %get-tuple-element.10, bf16[1,1024,3584]{2,1,0:T(8,128)(2,1)} %param.12), kind=kOutput, calls=%fused_computation.19 | convolution fusion | flops 2821324800 | bytes 16384000 | tf_op jit(solution)/shard_map/dot_general | solution.py:102
  138.2 0.2 pad_maximum_fusion
  138.4 38.0 %all_to_all.11 = bf16[16,24,3712]{2,1,0:T(8,128)(2,1)S(1)} all-to-all(bf16[16,24,3712]{2,1,0:T(8,128)(2,1)S(1)} %bitcast.92), channel_id=1, replica_groups=mesh['dp'=8,'expert'=16] {'expert'}, dimensions={0} | all-to-all | bytes 5701632 | tf_op jit(solution)/shard_map/all_to_all | solution.py:108
  176.4 0.1 slice_reduce_fusion
  176.5 0.2 fusion.36
  176.8 0.2 fusion.38
  177.0 0.5 pad_maximum_fusion.2
  177.5 1.6 convolution_convert_fusion.1
  179.1 63.2 %reduce-scatter.2.cloned.1.call-done = bf16[3,128,3584]{2,1,0:T(8,128)(2,1)} async-done(((bf16[3,1024,3584]{2,1,0:T(8,128)(2,1)}), bf16[3,128,3584]{2,1,0:T(8,128)(2,1)}) %reduce-scatter.2.cloned.1.call-update) | async-done | bytes 2752528 | tf_op jit(solution)/shard_map/reduce_scatter | solution.py:97
  242.4 3.3 %fusion.65 = (bf16[1,128,3584]{2,1,0:T(8,128)(2,1)}, bf16[1,128,3584]{2,1,0:T(8,128)(2,1)}, bf16[1,128,3584]{2,1,0:T(8,128)(2,1)}) fusion(bf16[3,128,3584]{2,1,0:T(8,128)(2,1)} %reduce-scatter.2.cloned.1.call-done), kind=kLoop, calls=%fused_computation.94 | loop fusion | bytes 5505024 | tf_op jit(solution)/shard_map/slice | solution.py:98
  (7 shorter events, 0.0 us)
Async XLA Ops:
  7.2 235.2 %reduce-scatter.2.cloned.1.call-start = ((), (), s32[]{:S(2)}) async-start(), calls=%async_computation.3 | async-start | bytes 24772608 | tf_op jit(solution)/shard_map/reduce_scatter | solution.py:97
  86.8 14.9 %slice-start = ((s8[7340032]{0:T(1024)(128)(4,1)}), s8[4194304]{0:T(1024)(128)(4,1)S(1)}, s32[]{:S(2)}) async-start(s8[7340032]{0:T(1024)(128)(4,1)} %bitcast.96), calls=%async_computation.4 | async-start | bytes 8388608
  94.2 7.4 %slice-start.1 = ((s8[7340032]{0:T(1024)(128)(4,1)}), s8[3145728]{0:T(1024)(128)(4,1)S(1)}, s32[]{:S(2)}) async-start(s8[7340032]{0:T(1024)(128)(4,1)} %bitcast.96), calls=%async_computation.5 | async-start | bytes 6291456
  125.2 1.1 copy-start
Sparse Core Ops, SparseCore 0:
  125.3 117.0 reduce-scatter.1

commit v8 on v7

--- a/solution.py
+++ b/solution.py
@@ -53,15 +53,15 @@
     slots = expert_count * capacity
     pair_table, token_table = build_tables(expert_ids, expert_count, capacity)
 
-    both = jnp.concatenate([inputs, out_grad], axis=1)
-    per_choice = jnp.stack(
-        [jnp.concatenate([both, lane_block(gates[:, k])], axis=1) for k in range(top_count)]
-    )
-    packed = lax.dot_general(
-        jnp.stack(pair_table),
-        per_choice,
-        (((0, 1), (0, 1)), ((), ())),
-        preferred_element_type=jnp.float32,
+    lane = lax.broadcasted_iota(jnp.int32, (token_count, LANES), 1)
+    choice_lanes = jnp.zeros((token_count, LANES), jnp.bfloat16)
+    for k in range(top_count):
+        choice_lanes = jnp.where(lane == k, gates[:, k][:, None], choice_lanes)
+        choice_lanes = jnp.where(
+            lane == top_count + k, expert_ids[:, k][:, None].astype(jnp.bfloat16), choice_lanes
+        )
+    packed = contract_rows(
+        token_table, jnp.concatenate([inputs, out_grad, choice_lanes], axis=1)
     ).astype(jnp.bfloat16)
     recv = lax.all_to_all(
         packed.reshape(expert_count, capacity, -1),
@@ -72,7 +72,12 @@
     ).reshape(slots, -1)
     row_inputs = recv[:, :width]
     row_out_grads = recv[:, width : 2 * width]
-    gate_col = recv[:, 2 * width : 2 * width + 1].astype(jnp.float32)
+    own = lax.axis_index("expert").astype(jnp.float32)
+    gate = recv[:, 2 * width + top_count - 1].astype(jnp.float32)
+    for k in range(top_count - 1):
+        named = recv[:, 2 * width + top_count + k].astype(jnp.float32)
+        gate = jnp.where(named == own, recv[:, 2 * width + k].astype(jnp.float32), gate)
+    gate_col = gate[:, None]
 
     gate_matrix = w_gate[0]
     up_matrix = w_up[0]

time: 253 us -> 288 us (1.14)
  waiting for transfers between devices: 63.2 us -> 150 us
  blocking collectives: 110 us -> 46 us
  starting transfers between devices: 0.04 us -> 7.84 us
    all_to_all x0 -> x1, waiting for transfers between devices: none -> 86.1 us  [shards(): lax.all_to_all(packed.reshape(expert_count, capacity, -1), 'expert', spli...]
    all_to_all x1 -> x0, blocking collectives: 72.3 us -> none  [shards(): lax.all_to_all(packed.reshape(expert_count, capacity, -1), 'expert', spli...]
    all_to_all x1, blocking collectives: 38 us -> 46 us  [shards(): lax.all_to_all(jnp.concatenate([row_back, value_block], axis=1).reshape(e...]
    all_to_all x0 -> x1, starting transfers between devices: none -> 7.62 us  [shards(): lax.all_to_all(packed.reshape(expert_count, capacity, -1), 'expert', spli...]
    dot_general x1, matrix products: 1.97 us -> 5.69 us  [contract_rows(): lax.dot_general(left, right, (((0,), (0,)), ((), ())), preferred_element_...]
  transfers between devices with their start and end apart: 1 -> 2, of which waited for: 1 -> 2; matrix products, arithmetic and copies ran while one was open for 6% -> 5% of each run, Pallas kernels for 0% -> 0%
where the time goes in v8:
time: 288 us; the launch traced here: 287 us
  waiting for transfers between devices  150 us (52%)
  matrix products  56 us (19%)
  blocking collectives  46 us (16%)
  between operations  14.2 us (5%)
  starting transfers between devices  7.84 us (3%)
  local copies, waits for them, and re-layouts  7.14 us (2%)
  other arithmetic  6.28 us (2%)
    all_to_all x1, waiting for transfers between devices, shards(): lax.all_to_all(packed.reshape(expert_count, capacity, -1), 'expert', spli...  86.1 us
    reduce_scatter x1, waiting for transfers between devices, shards(): joint = lax.psum_scatter(partials, 'dp', scatter_dimension=1, tiled=True)  63.4 us
    all_to_all x1, blocking collectives, shards(): lax.all_to_all(jnp.concatenate([row_back, value_block], axis=1).reshape(e...  46 us
    dot_general x3, matrix products, times_weight(): lax.dot_general(rows, weight, (((1,), (1,)), ((), ())), preferred_element...  19.2 us
    dot_general x1, matrix products, shards(): lax.dot_general(lefts, rights, (((1,), (1,)), ((0,), (0,))), preferred_el...  17.2 us
    all_to_all x1, starting transfers between devices, shards(): lax.all_to_all(packed.reshape(expert_count, capacity, -1), 'expert', spli...  7.62 us
    dot_general x1, matrix products, shards(): jnp.dot(up_hidden, up_matrix, preferred_element_type=jnp.float32)  6.47 us
  transfers between devices with their start and end apart: 2, of which 2 were waited for; matrix products, arithmetic and copies ran while one was open for 5% of the time, Pallas kernels for 0%

profile of v8, /device:TPU:1, one launch (start us, length us, event | category | flops | bytes accessed | tf_op | source)
XLA Modules:
  0.0 287.0 jit_solution(4038476477105775075)
XLA Ops:
  7.2 0.7 fusion.52
  7.9 0.2 fusion.53
  8.0 0.8 slice_bitcast_fusion.2
  8.8 0.8 fusion.61
  9.5 0.1 select_select_fusion
  9.7 5.7 %convolution_convert_fusion.1 = bf16[384,7296]{1,0:T(8,128)(2,1)} fusion(bf16[128,128]{1,0:T(8,128)(2,1)S(1)} %select_select_fusion, bf16[128,3584]{1,0:T(8,128)(2,1)} %param.8, bf16[128,3584]{1,0:T(8,128)(2,1)} %param.7, s32[128]{0:T(128)S(1)} %get-tuple-element.17, s32[128]{0:T(128)S(1)} %get-tuple-element.14), kind=kOutput, calls=%fused_computation.1 | convolution fusion | flops 726024192 | bytes 7472128 | tf_op jit(solution)/shard_map/dot_general | solution.py:29
  15.4 7.6 %all-to-all-start = ((bf16[16,24,7296]{2,1,0:T(8,128)(2,1)}), bf16[16,24,7296]{2,1,0:T(8,128)(2,1)}, u32[]{:S(2)}, u32[]{:S(2)}) async-start(bf16[16,24,7296]{2,1,0:T(8,128)(2,1)} %bitcast.82), calls=%async_computation | async-start | bytes 11206656 | tf_op jit(solution)/shard_map/all_to_all | solution.py:66
  23.0 0.2 reduce-scatter.2.cloned.1.call-start
  23.2 86.1 %all-to-all-done = bf16[16,24,7296]{2,1,0:T(8,128)(2,1)} async-done(((bf16[16,24,7296]{2,1,0:T(8,128)(2,1)}), bf16[16,24,7296]{2,1,0:T(8,128)(2,1)}, u32[]{:S(2)}, u32[]{:S(2)}) %all-to-all-start) | async-done | bytes 5603360 | tf_op jit(solution)/shard_map/all_to_all | solution.py:66
  109.3 2.0 slice_bitcast_fusion
  111.3 1.3 select_reduce_fusion
  112.5 2.6 fusion.21
  115.1 0.0 slice-start
  115.2 6.3 %fusion.11 = f32[384,1024]{1,0:T(8,128)S(1)} fusion(bf16[1,1024,3584]{2,1,0:T(8,128)(2,1)} %param.12, bf16[384,7296]{1,0:T(8,128)(2,1)} %bitcast.13), kind=kOutput, calls=%fused_computation.13 | convolution fusion | flops 2818572288 | bytes 11665408 | tf_op jit(solution)/shard_map/dot_general | solution.py:35
  121.5 0.0 slice-start.1
  121.5 6.3 %fusion.7 = f32[384,1024]{1,0:T(8,128)S(1)} fusion(bf16[1,1024,3584]{2,1,0:T(8,128)(2,1)} %param.11, bf16[384,7296]{1,0:T(8,128)(2,1)} %bitcast.13), kind=kOutput, calls=%fused_computation.9 | convolution fusion | flops 2818572288 | bytes 11665408 | tf_op jit(solution)/shard_map/dot_general | solution.py:35
  127.8 6.6 %multiply_reduce_fusion = (bf16[384]{0:T(512)(128)(2,1)S(1)}, bf16[384,1024]{1,0:T(8,128)(2,1)}, bf16[384,1024]{1,0:T(8,128)(2,1)}, bf16[384,1024]{1,0:T(8,128)(2,1)S(1)}) fusion(f32[384,1024]{1,0:T(8,128)S(1)} %fusion.11, f32[384,1024]{1,0:T(8,128)S(1)} %fusion.7, f32[384]{0:T(512)S(1)} %select_reduce_fusion, bf16[1,1024,3584]{2,1,0:T(8,128)(2,1)S(1)} %bitcast.87, ...), kind=kOutput, calls=%fused_computation.38 | convolution fusion | flops 2826436096 | bytes 15599872 | tf_op jit(solution)/shard_map/dot_general | solution.py:35
  134.5 17.2 %convolution_convert_fusion = bf16[3,1024,3584]{2,1,0:T(8,128)(2,1)} fusion(bf16[1,384,3584]{2,1,0:T(8,128)(2,1)S(1)} %fusion.21, bf16[1,384,3584]{2,1,0:T(8,128)(2,1)S(1)} %slice_bitcast_fusion, bf16[1,384,1024]{2,1,0:T(8,128)(2,1)} %bitcast.90, bf16[1,384,1024]{2,1,0:T(8,128)(2,1)S(1)} %bitcast.88, bf16[1,384,1024]{2,1,0:T(8,128)(2,1)} %bitcast.89), kind=kOutput, calls=%fused_computation | convolution fusion | flops 8477343744 | bytes 29884416 | tf_op jit(solution)/shard_map/dot_general | solution.py:99
  151.6 0.0 reduce-scatter.2.cloned.1.call-update
  151.7 0.1 broadcast_select_fusion
  151.8 1.0 copy-done
  152.8 5.2 %fusion.5 = f32[384,3584]{1,0:T(8,128)S(1)} fusion(bf16[384,1024]{1,0:T(8,128)(2,1)S(1)} %copy-done, bf16[1,1024,3584]{2,1,0:T(8,128)(2,1)} %param.11), kind=kOutput, calls=%fused_computation.7 | convolution fusion | flops 2818572288 | bytes 13631488 | tf_op jit(solution)/shard_map/dot_general | solution.py:106
  158.0 6.5 %fusion.18 = bf16[384,3584]{1,0:T(8,128)(2,1)S(1)} fusion(f32[384,3584]{1,0:T(8,128)S(1)} %fusion.5, bf16[384,1024]{1,0:T(8,128)(2,1)S(1)} %get-tuple-element.10, bf16[1,1024,3584]{2,1,0:T(8,128)(2,1)} %param.12), kind=kOutput, calls=%fused_computation.18 | convolution fusion | flops 2821324800 | bytes 16384000 | tf_op jit(solution)/shard_map/dot_general | solution.py:107
  164.5 0.2 pad_maximum_fusion
  164.7 46.0 %all_to_all.10 = bf16[16,24,3712]{2,1,0:T(8,128)(2,1)S(1)} all-to-all(bf16[16,24,3712]{2,1,0:T(8,128)(2,1)S(1)} %bitcast.83), channel_id=1, replica_groups=mesh['dp'=8,'expert'=16] {'expert'}, dimensions={0} | all-to-all | bytes 5701632 | tf_op jit(solution)/shard_map/all_to_all | solution.py:113
  210.7 0.1 slice_reduce_fusion
  210.8 0.2 fusion.37
  211.0 0.2 fusion.39
  211.3 0.5 pad_maximum_fusion.1
  211.8 1.6 convolution_convert_fusion.2
  213.4 63.4 %reduce-scatter.2.cloned.1.call-done = bf16[3,128,3584]{2,1,0:T(8,128)(2,1)} async-done(((bf16[3,1024,3584]{2,1,0:T(8,128)(2,1)}), bf16[3,128,3584]{2,1,0:T(8,128)(2,1)}) %reduce-scatter.2.cloned.1.call-update) | async-done | bytes 2752528 | tf_op jit(solution)/shard_map/reduce_scatter | solution.py:102
  276.9 3.3 %fusion.64 = (bf16[1,128,3584]{2,1,0:T(8,128)(2,1)}, bf16[1,128,3584]{2,1,0:T(8,128)(2,1)}, bf16[1,128,3584]{2,1,0:T(8,128)(2,1)}) fusion(bf16[3,128,3584]{2,1,0:T(8,128)(2,1)} %reduce-scatter.2.cloned.1.call-done), kind=kLoop, calls=%fused_computation.93 | loop fusion | bytes 5505024 | tf_op jit(solution)/shard_map/slice | solution.py:103
  (7 shorter events, 0.0 us)
Async XLA Ops:
  15.4 94.0 %all-to-all-start = ((bf16[16,24,7296]{2,1,0:T(8,128)(2,1)}), bf16[16,24,7296]{2,1,0:T(8,128)(2,1)}, u32[]{:S(2)}, u32[]{:S(2)}) async-start(bf16[16,24,7296]{2,1,0:T(8,128)(2,1)} %bitcast.82), calls=%async_computation | async-start | bytes 11206656 | tf_op jit(solution)/shard_map/all_to_all | solution.py:66
  23.0 253.9 %reduce-scatter.2.cloned.1.call-start = ((), (), s32[]{:S(2)}) async-start(), calls=%async_computation.3 | async-start | bytes 24772608 | tf_op jit(solution)/shard_map/reduce_scatter | solution.py:102
  115.1 12.6 %slice-start = ((s8[7340032]{0:T(1024)(128)(4,1)}), s8[4194304]{0:T(1024)(128)(4,1)S(1)}, s32[]{:S(2)}) async-start(s8[7340032]{0:T(1024)(128)(4,1)} %bitcast.86), calls=%async_computation.4 | async-start | bytes 8388608
  121.5 6.3 %slice-start.1 = ((s8[7340032]{0:T(1024)(128)(4,1)}), s8[3145728]{0:T(1024)(128)(4,1)S(1)}, s32[]{:S(2)}) async-start(s8[7340032]{0:T(1024)(128)(4,1)} %bitcast.86), calls=%async_computation.5 | async-start | bytes 6291456
  151.6 1.1 copy-start
Sparse Core Ops, SparseCore 0:
  151.8 125.0 reduce-scatter.1
